TPU v7x, 32 devices: a whole 2x2x4 slice. The times are simulated.
32 devices in a mesh: blk: 4 (over y, core), grp: 8 (over z, x).
Axes of the slice: x: 2, y: 2, z: 4, core: 2. Of those that a mesh axis runs over, the one named last changes fastest.
Arguments:
- features: bfloat16 [4096, 256], P(('blk', 'grp')), may hold values from -6 to 6
- weights: bfloat16 [2, 256, 256], replicated, may hold values from -0.375 to 0.375
- biases: float32 [2, 256], replicated, may hold values from -0.6 to 0.6
- adjacency: bfloat16 [4, 8, 6, 256, 256], P('blk', 'grp'), as said below
- tile_row: int32 [4, 8, 6], P('blk', 'grp'), may hold values from 0 to 1
- tile_column: int32 [4, 8, 6], P('blk', 'grp'), may hold values from 0 to 3
- tile_count: int32 [4, 8], P('blk', 'grp'), may hold values from 1 to 6, as said below
Outputs:
- result: bfloat16 [4096, 256], P(('blk', 'grp'))
Inputs may be any that keep to these rules, and one draw needn't show every extreme that they name: tile_count is at least 1 and at most 6; some device has exactly 6 live slots. `adjacency`: edge weights are zero or positive.
All inputs are finite; a program needn't handle non-finite values.
Results may differ from a plain program's by a relative error of at most 0.0046.
Values may be sent and summed in bfloat16 or wider, within the bound.
No kernel may reach another device: no remote copies, remote signals or barrier semaphores. Data moves between devices by JAX's collectives and lax.ppermute only.
A program may use at most 64 MiB of HBM per device.

v0:
```python
import jax
import jax.numpy as jnp
from jax import lax
from jax.sharding import PartitionSpec as P

LAYERS = 2


def aggregate(adjacency, cols_here, placing, column_rows, row_tiles):
    tile_size = adjacency.shape[1]
    width = column_rows.shape[1]
    blocks = column_rows.reshape(-1, tile_size, width)[cols_here]
    product = jnp.einsum("tij,tjf->tif", adjacency, blocks, preferred_element_type=jnp.float32)
    placed = jnp.einsum("rt,tif->rif", placing, product, precision=lax.Precision.HIGHEST)
    return placed.reshape(row_tiles * tile_size, width)


def on_device(features, weights, biases, adjacency, tile_row, tile_column, tile_count):
    adjacency = adjacency[0, 0]
    rows_here = tile_row[0, 0]
    cols_here = tile_column[0, 0]
    count_here = tile_count[0, 0]
    blk_size = lax.axis_size("blk")
    node_dev = features.shape[0]
    tile_size = adjacency.shape[1]
    slots = adjacency.shape[0]
    width = features.shape[1]
    row_tiles = blk_size * node_dev // tile_size
    live = lax.iota(jnp.int32, slots) < count_here
    placing = (
        (rows_here[None, :] == lax.iota(jnp.int32, row_tiles)[:, None]) & live[None, :]
    ).astype(jnp.float32)
    row_sums = jnp.sum(adjacency, axis=2, dtype=jnp.float32)
    degree_part = jnp.dot(placing, row_sums, precision=lax.Precision.HIGHEST).reshape(
        blk_size, node_dev
    )
    degree = lax.psum_scatter(degree_part, "blk", scatter_dimension=0, tiled=True)[0]
    scale = lax.rsqrt(1.0 + degree)[:, None]
    hidden = features
    result = None
    for layer_index in range(LAYERS):
        mixed = jnp.dot(hidden, weights[layer_index], preferred_element_type=jnp.float32)
        scaled = (mixed * scale).astype(jnp.bfloat16)
        column_rows = lax.all_gather(scaled, "grp", axis=0, tiled=True)
        partial_value = aggregate(adjacency, cols_here, placing, column_rows, row_tiles)
        partial_value = partial_value.reshape(blk_size, node_dev, width)
        summed = lax.psum_scatter(partial_value, "blk", scatter_dimension=0, tiled=True)[0]
        pre = (summed + scaled.astype(jnp.float32)) * scale + biases[layer_index][None, :]
        if layer_index < LAYERS - 1:
            hidden = jnp.maximum(pre, 0.0).astype(jnp.bfloat16)
        else:
            result = pre.astype(jnp.bfloat16)
    return result


def solution(mesh):
    placed = (
        P(("blk", "grp"), None),
        P(),
        P(),
        P("blk", "grp", None, None, None),
        P("blk", "grp", None),
        P("blk", "grp", None),
        P("blk", "grp"),
    )
    return jax.shard_map(
        on_device, mesh=mesh, in_specs=placed, out_specs=P(("blk", "grp"), None), check_vma=False
    )
```

profile of v0, /device:TPU:0, one launch (start us, length us, event | category | flops | bytes accessed | tf_op | source)
XLA Modules:
  0.0 150.4 jit_solution(8604493189462942408)
XLA Ops:
  7.3 1.4 convert_reduce_fusion
  8.7 0.8 fusion.31
  9.5 8.4 %all-reduce = f32[4,128]{1,0:T(4,128)S(1)} all-reduce(f32[4,128]{1,0:T(4,128)S(1)} %reshape.51), channel_id=2, replica_groups=mesh['blk'=4,'grp'=8] {'blk'}, use_global_device_ids=true, to_apply=%region_1.0.clone | all-reduce | flops 512 | bytes 4096
  17.9 1.2 dynamic-slice
  19.1 0.7 fusion.29
  19.8 1.1 fusion.4
  20.8 31.9 %all_gather.6 = bf16[1024,256]{1,0:T(8,128)(2,1)S(1)} all-gather(bf16[128,256]{1,0:T(8,128)(2,1)S(1)} %fusion.4), channel_id=1, replica_groups=mesh['blk'=4,'grp'=8] {'grp'}, dimensions={0}, use_global_device_ids=true | all-gather | bytes 589824 | tf_op jit(solution)/shard_map/all_gather | solution.py:44
  52.7 0.7 fusion.27
  53.4 0.6 gather_fusion
  54.0 1.6 %fusion.8 = f32[6,256,256]{2,1,0:T(8,128)} fusion(bf16[6,256,256]{2,1,0:T(8,128)(2,1)S(1)} %gather_fusion, bf16[1,1,6,256,256]{4,3,2,1,0:T(8,128)(2,1)S(1)} %copy-done.1), kind=kOutput, calls=%fused_computation.13 | convolution fusion | flops 201326592 | bytes 3145728 | tf_op jit(solution)/shard_map/tij,tjf->tif/dot_general | solution.py:13
  55.6 2.1 %copy.12 = f32[6,256,256]{1,0,2:T(8,128)S(1)} copy(f32[6,256,256]{2,1,0:T(8,128)} %fusion.8) | data formatting | bytes 3145728 | tf_op jit(solution)/shard_map/tij,tjf->tif/dot_general | solution.py:13
  57.7 1.1 fusion.2
  58.8 0.8 copy.10
  59.7 0.0 reduce-scatter.5.cloned.1.call-start
  59.7 21.6 %reduce-scatter.3.cloned.1.call-done = f32[1,128,256]{2,1,0:T(8,128)} async-done(((f32[4,128,256]{2,1,0:T(8,128)}), f32[1,128,256]{2,1,0:T(8,128)}) %reduce-scatter.3.cloned.1.call-update) | async-done | bytes 131088 | tf_op jit(solution)/shard_map/reduce_scatter | solution.py:47
  81.4 1.1 fusion.5
  82.5 31.3 %all_gather.7 = bf16[1024,256]{1,0:T(8,128)(2,1)S(1)} all-gather(bf16[128,256]{1,0:T(8,128)(2,1)S(1)} %fusion.5), channel_id=1, replica_groups=mesh['blk'=4,'grp'=8] {'grp'}, dimensions={0}, use_global_device_ids=true | all-gather | bytes 589824 | tf_op jit(solution)/shard_map/all_gather | solution.py:44
  113.8 0.6 gather_fusion.1
  114.4 1.6 %fusion.6 = f32[6,256,256]{2,1,0:T(8,128)} fusion(bf16[6,256,256]{2,1,0:T(8,128)(2,1)S(1)} %gather_fusion.1, bf16[1,1,6,256,256]{4,3,2,1,0:T(8,128)(2,1)S(1)} %copy-done.1), kind=kOutput, calls=%fused_computation.11 | convolution fusion | flops 201326592 | bytes 3145728 | tf_op jit(solution)/shard_map/tij,tjf->tif/dot_general | solution.py:13
  116.0 2.1 %copy.13 = f32[6,256,256]{1,0,2:T(8,128)S(1)} copy(f32[6,256,256]{2,1,0:T(8,128)} %fusion.6) | data formatting | bytes 3145728 | tf_op jit(solution)/shard_map/tij,tjf->tif/dot_general | solution.py:13
  118.1 1.1 fusion
  119.2 0.8 copy.11
  120.0 21.9 %reduce-scatter.5.cloned.1.call-done = f32[1,128,256]{2,1,0:T(8,128)} async-done(((f32[4,128,256]{2,1,0:T(8,128)}), f32[1,128,256]{2,1,0:T(8,128)}) %reduce-scatter.5.cloned.1.call-update) | async-done | bytes 131088 | tf_op jit(solution)/shard_map/reduce_scatter | solution.py:47
  141.9 1.6 %fusion.12 = bf16[128,256]{1,0:T(8,128)(2,1)} fusion(f32[1,128,256]{2,1,0:T(8,128)} %reduce-scatter.5.cloned.1.call-done, bf16[128,256]{1,0:T(8,128)(2,1)S(1)} %fusion.5, f32[256]{0:T(256)S(1)} %bitcast.69, f32[128]{0:T(128)S(1)} %fusion.29), kind=kLoop, calls=%fused_computation.18 | loop fusion | flops 163840 | bytes 263680 | tf_op jit(solution)/shard_map/convert_element_type | solution.py:52
  (17 shorter events, 0.1 us)
Async XLA Ops:
  6.5 13.2 %copy-start = (bf16[128,256]{1,0:T(8,128)(2,1)S(1)}, bf16[128,256]{1,0:T(8,128)(2,1)}, u32[]{:S(2)}) copy-start(bf16[128,256]{1,0:T(8,128)(2,1)} %param.7) | copy-start | bytes 196612
  6.5 47.4 %copy-start.1 = (bf16[1,1,6,256,256]{4,3,2,1,0:T(8,128)(2,1)S(1)}, bf16[1,1,6,256,256]{4,3,2,1,0:T(8,128)(2,1)}, u32[]{:S(2)}) copy-start(bf16[1,1,6,256,256]{4,3,2,1,0:T(8,128)(2,1)} %param.10) | copy-start | bytes 2359300
  6.5 74.8 %reduce-scatter.3.cloned.1.call-start = ((), (), s32[]{:S(2)}) async-start(), calls=%async_computation.2 | async-start | bytes 655360 | tf_op jit(solution)/shard_map/reduce_scatter | solution.py:47
  55.6 2.1 %copy-start.3 = (s32[1,1,6]{2,1,0:T(1,128)S(1)}, s32[1,1,6]{2,1,0:T(1,128)}, u32[]{:S(2)}) copy-start(s32[1,1,6]{2,1,0:T(1,128)} %param.11) | copy-start | bytes 76
  57.7 2.0 %copy-start.4 = (f32[2,256]{1,0:T(2,128)S(1)}, f32[2,256]{1,0:T(2,128)}, u32[]{:S(2)}) copy-start(f32[2,256]{1,0:T(2,128)} %param.9) | copy-start | bytes 6148
  57.7 23.6 %copy-start.2 = (bf16[2,256,256]{2,1,0:T(8,128)(2,1)S(1)}, bf16[2,256,256]{2,1,0:T(8,128)(2,1)}, u32[]{:S(2)}) copy-start(bf16[2,256,256]{2,1,0:T(8,128)(2,1)} %param.8) | copy-start | bytes 786436
  59.7 82.3 %reduce-scatter.5.cloned.1.call-start = ((), (), s32[]{:S(2)}) async-start(), calls=%async_computation.3 | async-start | bytes 655360 | tf_op jit(solution)/shard_map/reduce_scatter | solution.py:47
Sparse Core Ops, SparseCore 0:
  59.8 21.5 reduce-scatter.2
  120.1 21.7 reduce-scatter.4
where the time goes:
time: 151 us; the launch traced here: 150 us
  blocking collectives  71.6 us (47%)
  waiting for transfers between devices  43.6 us (29%)
  between operations  14.3 us (9%)
  local copies, waits for them, and re-layouts  8.33 us (6%)
  matrix products  8.28 us (5%)
  other arithmetic  4.35 us (3%)
    all_gather x2, blocking collectives, on_device(): column_rows = lax.all_gather(scaled, 'grp', axis=0, tiled=True)  63.2 us
    reduce_scatter x2, waiting for transfers between devices, on_device(): lax.psum_scatter(partial_value, 'blk', scatter_dimension=0, tiled=True)[0]  43.5 us
    unnamed x1, blocking collectives  8.36 us
    dot_general x2, local copies, waits for them, and re-layouts, aggregate(): jnp.einsum('tij,tjf->tif', adjacency, blocks, preferred_element_type=jnp....  4.21 us
    dot_general x2, matrix products, aggregate(): jnp.einsum('tij,tjf->tif', adjacency, blocks, preferred_element_type=jnp....  3.17 us
  transfers between devices with their start and end apart: 2, of which 2 were waited for; matrix products, arithmetic and copies ran while one was open for 0% of the time, Pallas kernels for 0%

commit v1 on v0

v1 whole, which is shorter than its diff:
```python
import jax
import jax.numpy as jnp
from jax import lax
from jax.sharding import PartitionSpec as P

LAYERS = 2


def gather_group(block, axis, size):
    received = [block]
    for shift in range(1, size):
        perm = [(i, (i - shift) % size) for i in range(size)]
        received.append(lax.ppermute(block, axis, perm=perm))
    return jnp.stack(received)


def scatter_sum(parts, axis, size):
    me = lax.axis_index(axis)
    total = lax.dynamic_index_in_dim(parts, me, 0, keepdims=False)
    for shift in range(1, size):
        perm = [(i, (i + shift) % size) for i in range(size)]
        outgoing = lax.dynamic_index_in_dim(parts, (me + shift) % size, 0, keepdims=False)
        total = total + lax.ppermute(outgoing, axis, perm=perm)
    return total


def on_device(features, weights, biases, adjacency, tile_row, tile_column, tile_count):
    adjacency = adjacency[0, 0]
    rows_here = tile_row[0, 0]
    cols_here = tile_column[0, 0]
    count_here = tile_count[0, 0]
    blk_size = lax.axis_size("blk")
    grp_size = lax.axis_size("grp")
    node_dev = features.shape[0]
    tile_size = adjacency.shape[1]
    slots = adjacency.shape[0]
    width = features.shape[1]
    row_tiles = blk_size * node_dev // tile_size
    per_tile = tile_size // node_dev
    live = lax.iota(jnp.int32, slots) < count_here
    placing = (
        (rows_here[None, :] == lax.iota(jnp.int32, row_tiles)[:, None]) & live[None, :]
    ).astype(jnp.float32)
    row_sums = jnp.sum(adjacency, axis=2, dtype=jnp.float32)
    degree_part = jnp.dot(placing, row_sums, precision=lax.Precision.HIGHEST).reshape(
        blk_size, node_dev
    )
    degree = scatter_sum(degree_part, "blk", blk_size)
    scale = lax.rsqrt(1.0 + degree)[:, None]
    me_grp = lax.axis_index("grp")
    sources = cols_here[:, None] * per_tile + lax.iota(jnp.int32, per_tile)[None, :]
    slot_of_source = (sources - me_grp) % grp_size
    hidden = features
    result = None
    for layer_index in range(LAYERS):
        mixed = jnp.dot(hidden, weights[layer_index], preferred_element_type=jnp.float32)
        scaled = (mixed * scale).astype(jnp.bfloat16)
        received = gather_group(scaled, "grp", grp_size)
        blocks = received[slot_of_source].reshape(slots, tile_size, width)
        product = jnp.einsum("tij,tjf->tif", adjacency, blocks, preferred_element_type=jnp.float32)
        placed = jnp.einsum("rt,tif->rif", placing, product, precision=lax.Precision.HIGHEST)
        partial_value = placed.reshape(blk_size, node_dev, width)
        summed = scatter_sum(partial_value, "blk", blk_size)
        pre = (summed + scaled.astype(jnp.float32)) * scale + biases[layer_index][None, :]
        if layer_index < LAYERS - 1:
            hidden = jnp.maximum(pre, 0.0).astype(jnp.bfloat16)
        else:
            result = pre.astype(jnp.bfloat16)
    return result


def solution(mesh):
    placed = (
        P(("blk", "grp"), None),
        P(),
        P(),
        P("blk", "grp", None, None, None),
        P("blk", "grp", None),
        P("blk", "grp", None),
        P("blk", "grp"),
    )
    return jax.shard_map(
        on_device, mesh=mesh, in_specs=placed, out_specs=P(("blk", "grp"), None), check_vma=False
    )
```

time: 151 us -> 72.7 us (0.48)
  blocking collectives: 71.6 us -> 0 us
  starting transfers between devices: 0.04 us -> 29.7 us
  waiting for transfers between devices: 43.6 us -> 24.7 us
  between operations: 14.3 us -> 1.01 us
  local copies, waits for them, and re-layouts: 8.33 us -> 5.76 us
    all_gather x2 -> x0, blocking collectives: 63.2 us -> none  [on_device(): column_rows = lax.all_gather(scaled, 'grp', axis=0, tiled=True)]
    reduce_scatter x2 -> x0, waiting for transfers between devices: 43.5 us -> none  [on_device(): lax.psum_scatter(partial_value, 'blk', scatter_dimension=0, tiled=True)[0]]
    ppermute x0 -> x23, starting transfers between devices: none -> 29.7 us  [the longest x14 19.8 us: gather_group(): received.append(lax.ppermute(block, axis, perm=perm))]
    ppermute x0 -> x23, waiting for transfers between devices: none -> 24.7 us  [the longest x14 14.9 us: gather_group(): received.append(lax.ppermute(block, axis, perm=perm))]
    unnamed x1 -> x0, blocking collectives: 8.36 us -> none
    dot_general x4, local copies, waits for them, and re-layouts: 5.85 us -> 4.28 us  [the longest x2 4.21 us: on_device(): jnp.einsum('tij,tjf->tif', adjacency, blocks, preferred_element_type=jnp....]
  transfers between devices with their start and end apart: 2 -> 23, of which waited for: 2 -> 11; matrix products, arithmetic and copies ran while one was open for 0% -> 1% of each run, Pallas kernels for 0% -> 0%
where the time goes in v1:
time: 72.7 us; the launch traced here: 71.5 us
  starting transfers between devices  29.7 us (41%)
  waiting for transfers between devices  24.7 us (34%)
  matrix products  7.47 us (10%)
  local copies, waits for them, and re-layouts  5.76 us (8%)
  other arithmetic  2.89 us (4%)
  between operations  1.01 us (1%)
    ppermute x14, starting transfers between devices, gather_group(): received.append(lax.ppermute(block, axis, perm=perm))  19.8 us
    ppermute x14, waiting for transfers between devices, gather_group(): received.append(lax.ppermute(block, axis, perm=perm))  14.9 us
    ppermute x9, starting transfers between devices, scatter_sum(): total = total + lax.ppermute(outgoing, axis, perm=perm)  9.92 us
    ppermute x9, waiting for transfers between devices, scatter_sum(): total = total + lax.ppermute(outgoing, axis, perm=perm)  9.78 us
    dot_general x2, local copies, waits for them, and re-layouts, on_device(): jnp.einsum('tij,tjf->tif', adjacency, blocks, preferred_element_type=jnp....  4.21 us
    dot_general x2, matrix products, on_device(): jnp.einsum('tij,tjf->tif', adjacency, blocks, preferred_element_type=jnp....  3.25 us
    dot_general x2, matrix products, on_device(): jnp.einsum('rt,tif->rif', placing, product, precision=lax.Precision.HIGHEST)  2.16 us
  transfers between devices with their start and end apart: 23, of which 11 were waited for; matrix products, arithmetic and copies ran while one was open for 1% of the time, Pallas kernels for 0%

profile of v1, /device:TPU:0, one launch (start us, length us, event | category | flops | bytes accessed | tf_op | source)
XLA Modules:
  0.0 71.5 jit_solution(5115400104682084232)
XLA Ops:
  0.7 1.4 %convert_reduce_fusion = f32[6,256]{1,0:T(8,128)S(1)} fusion(bf16[1,1,6,256,256]{4,3,2,1,0:T(8,128)(2,1)} %param.10), kind=kLoop, calls=%fused_computation.6 | loop fusion | flops 784896 | bytes 792576 | tf_op jit(solution)/shard_map/reduce_sum | solution.py:44
  3.5 2.6 %collective-permute-start.1 = (f32[128]{0:T(128)S(1)}, f32[128]{0:T(128)S(1)}, u32[]{:S(2)}, u32[]{:S(2)}) collective-permute-start(f32[128]{0:T(128)S(1)} %get-tuple-element.15), channel_id=1, source_target_pairs={{0,16},{8,24},{16,0},{24,8},{1,17},{9,25},{17,1},{25,9},{2,18},{10... | collective-permute-start | bytes 1544 | tf_op jit(solution)/shard_map/ppermute | solution.py:23
  6.1 1.4 %collective-permute-start.2 = (f32[128]{0:T(128)S(1)}, f32[128]{0:T(128)S(1)}, u32[]{:S(2)}, u32[]{:S(2)}) collective-permute-start(f32[128]{0:T(128)S(1)} %get-tuple-element.14), channel_id=1, source_target_pairs={{0,24},{8,0},{16,8},{24,16},{1,25},{9,1},{17,9},{25,17},{2,26},{10... | collective-permute-start | bytes 1544 | tf_op jit(solution)/shard_map/ppermute | solution.py:23
  9.9 4.6 %collective-permute-start.3 = (bf16[128,256]{1,0:T(8,128)(2,1)S(1)}, bf16[128,256]{1,0:T(8,128)(2,1)S(1)}, u32[]{:S(2)}, u32[]{:S(2)}) collective-permute-start(bf16[128,256]{1,0:T(8,128)(2,1)S(1)} %get-tuple-element.17), channel_id=1, source_target_pairs={{0,7},{1,0},{2,1},{3,2},{4,3},{5,4},{6,5},{7,6},{8,15},{9,8},{10,9... | collective-permute-start | bytes 196616 | tf_op jit(solution)/shard_map/ppermute | solution.py:13
  14.9 3.0 %collective-permute-start.6 = (bf16[128,256]{1,0:T(8,128)(2,1)S(1)}, bf16[128,256]{1,0:T(8,128)(2,1)S(1)}, u32[]{:S(2)}, u32[]{:S(2)}) collective-permute-start(bf16[128,256]{1,0:T(8,128)(2,1)S(1)} %get-tuple-element.17), channel_id=1, source_target_pairs={{0,4},{1,5},{2,6},{3,7},{4,0},{5,1},{6,2},{7,3},{8,12},{9,13},{10,... | collective-permute-start | bytes 196616 | tf_op jit(solution)/shard_map/ppermute | solution.py:13
  17.9 1.8 %collective-permute-start.8 = (bf16[128,256]{1,0:T(8,128)(2,1)S(1)}, bf16[128,256]{1,0:T(8,128)(2,1)S(1)}, u32[]{:S(2)}, u32[]{:S(2)}) collective-permute-start(bf16[128,256]{1,0:T(8,128)(2,1)S(1)} %get-tuple-element.17), channel_id=1, source_target_pairs={{0,2},{1,3},{2,4},{3,5},{4,6},{5,7},{6,0},{7,1},{8,10},{9,11},{10,... | collective-permute-start | bytes 196616 | tf_op jit(solution)/shard_map/ppermute | solution.py:13
  21.0 5.9 %collective-permute-done.6 = bf16[128,256]{1,0:T(8,128)(2,1)S(1)} collective-permute-done((bf16[128,256]{1,0:T(8,128)(2,1)S(1)}, bf16[128,256]{1,0:T(8,128)(2,1)S(1)}, u32[]{:S(2)}, u32[]{:S(2)}) %collective-permute-start.6) | collective-permute-done | bytes 65568 | tf_op jit(solution)/shard_map/ppermute | solution.py:13
  26.9 2.3 %collective-permute-done.7 = bf16[128,256]{1,0:T(8,128)(2,1)S(1)} collective-permute-done((bf16[128,256]{1,0:T(8,128)(2,1)S(1)}, bf16[128,256]{1,0:T(8,128)(2,1)S(1)}, u32[]{:S(2)}, u32[]{:S(2)}) %collective-permute-start.7) | collective-permute-done | bytes 65568 | tf_op jit(solution)/shard_map/ppermute | solution.py:13
  29.9 1.6 %fusion.8 = f32[6,256,256]{2,1,0:T(8,128)} fusion(bf16[6,256,256]{2,1,0:T(8,128)(2,1)S(1)} %bitcast.138, bf16[1,1,6,256,256]{4,3,2,1,0:T(8,128)(2,1)S(1)} %copy-done.1), kind=kOutput, calls=%fused_computation.13 | convolution fusion | flops 201326592 | bytes 3145728 | tf_op jit(solution)/shard_map/tij,tjf->tif/dot_general | solution.py:60
  31.5 2.1 %copy.10 = f32[6,256,256]{1,0,2:T(8,128)S(1)} copy(f32[6,256,256]{2,1,0:T(8,128)} %fusion.8) | data formatting | bytes 3145728 | tf_op jit(solution)/shard_map/tij,tjf->tif/dot_general | solution.py:60
  34.9 1.6 %collective-permute-start.11 = (f32[128,256]{1,0:T(8,128)S(1)}, f32[128,256]{1,0:T(8,128)S(1)}, u32[]{:S(2)}, u32[]{:S(2)}) collective-permute-start(f32[128,256]{1,0:T(8,128)S(1)} %get-tuple-element.10), channel_id=1, source_target_pairs={{0,16},{8,24},{16,0},{24,8},{1,17},{9,25},{17,1},{25,9},{2,18},{10... | collective-permute-start | bytes 393224 | tf_op jit(solution)/shard_map/ppermute | solution.py:23
  36.5 1.4 %collective-permute-start.12 = (f32[128,256]{1,0:T(8,128)S(1)}, f32[128,256]{1,0:T(8,128)S(1)}, u32[]{:S(2)}, u32[]{:S(2)}) collective-permute-start(f32[128,256]{1,0:T(8,128)S(1)} %get-tuple-element.9), channel_id=1, source_target_pairs={{0,24},{8,0},{16,8},{24,16},{1,25},{9,1},{17,9},{25,17},{2,26},{10... | collective-permute-start | bytes 393224 | tf_op jit(solution)/shard_map/ppermute | solution.py:23
  37.9 2.2 %collective-permute-done.10 = f32[128,256]{1,0:T(8,128)S(1)} collective-permute-done((f32[128,256]{1,0:T(8,128)S(1)}, f32[128,256]{1,0:T(8,128)S(1)}, u32[]{:S(2)}, u32[]{:S(2)}) %collective-permute-start.10) | collective-permute-done | bytes 131104 | tf_op jit(solution)/shard_map/ppermute | solution.py:23
  41.3 1.2 %collective-permute-done.12 = f32[128,256]{1,0:T(8,128)S(1)} collective-permute-done((f32[128,256]{1,0:T(8,128)S(1)}, f32[128,256]{1,0:T(8,128)S(1)}, u32[]{:S(2)}, u32[]{:S(2)}) %collective-permute-start.12) | collective-permute-done | bytes 131104 | tf_op jit(solution)/shard_map/ppermute | solution.py:23
  42.8 1.2 %collective-permute-start.14 = (bf16[128,256]{1,0:T(8,128)(2,1)S(1)}, bf16[128,256]{1,0:T(8,128)(2,1)S(1)}, u32[]{:S(2)}, u32[]{:S(2)}) collective-permute-start(bf16[128,256]{1,0:T(8,128)(2,1)S(1)} %get-tuple-element.19), channel_id=1, source_target_pairs={{0,6},{1,7},{2,0},{3,1},{4,2},{5,3},{6,4},{7,5},{8,14},{9,15},{10,... | collective-permute-start | bytes 196616 | tf_op jit(solution)/shard_map/ppermute | solution.py:13
  45.0 2.2 %collective-permute-start.16 = (bf16[128,256]{1,0:T(8,128)(2,1)S(1)}, bf16[128,256]{1,0:T(8,128)(2,1)S(1)}, u32[]{:S(2)}, u32[]{:S(2)}) collective-permute-start(bf16[128,256]{1,0:T(8,128)(2,1)S(1)} %get-tuple-element.19), channel_id=1, source_target_pairs={{0,4},{1,5},{2,6},{3,7},{4,0},{5,1},{6,2},{7,3},{8,12},{9,13},{10,... | collective-permute-start | bytes 196616 | tf_op jit(solution)/shard_map/ppermute | solution.py:13
  48.2 1.3 %collective-permute-start.18 = (bf16[128,256]{1,0:T(8,128)(2,1)S(1)}, bf16[128,256]{1,0:T(8,128)(2,1)S(1)}, u32[]{:S(2)}, u32[]{:S(2)}) collective-permute-start(bf16[128,256]{1,0:T(8,128)(2,1)S(1)} %get-tuple-element.19), channel_id=1, source_target_pairs={{0,2},{1,3},{2,4},{3,5},{4,6},{5,7},{6,0},{7,1},{8,10},{9,11},{10,... | collective-permute-start | bytes 196616 | tf_op jit(solution)/shard_map/ppermute | solution.py:13
  49.5 2.0 %collective-permute-start.19 = (bf16[128,256]{1,0:T(8,128)(2,1)S(1)}, bf16[128,256]{1,0:T(8,128)(2,1)S(1)}, u32[]{:S(2)}, u32[]{:S(2)}) collective-permute-start(bf16[128,256]{1,0:T(8,128)(2,1)S(1)} %get-tuple-element.19), channel_id=1, source_target_pairs={{0,1},{1,2},{2,3},{3,4},{4,5},{5,6},{6,7},{7,0},{8,9},{9,10},{10,1... | collective-permute-start | bytes 196616 | tf_op jit(solution)/shard_map/ppermute | solution.py:13
  51.5 5.2 %collective-permute-done.16 = bf16[128,256]{1,0:T(8,128)(2,1)S(1)} collective-permute-done((bf16[128,256]{1,0:T(8,128)(2,1)S(1)}, bf16[128,256]{1,0:T(8,128)(2,1)S(1)}, u32[]{:S(2)}, u32[]{:S(2)}) %collective-permute-start.16) | collective-permute-done | bytes 65568 | tf_op jit(solution)/shard_map/ppermute | solution.py:13
  56.7 1.5 %collective-permute-done.17 = bf16[128,256]{1,0:T(8,128)(2,1)S(1)} collective-permute-done((bf16[128,256]{1,0:T(8,128)(2,1)S(1)}, bf16[128,256]{1,0:T(8,128)(2,1)S(1)}, u32[]{:S(2)}, u32[]{:S(2)}) %collective-permute-start.17) | collective-permute-done | bytes 65568 | tf_op jit(solution)/shard_map/ppermute | solution.py:13
  58.8 1.6 %fusion.6 = f32[6,256,256]{2,1,0:T(8,128)} fusion(bf16[6,256,256]{2,1,0:T(8,128)(2,1)S(1)} %bitcast.137, bf16[1,1,6,256,256]{4,3,2,1,0:T(8,128)(2,1)S(1)} %copy-done.1), kind=kOutput, calls=%fused_computation.11 | convolution fusion | flops 201326592 | bytes 3145728 | tf_op jit(solution)/shard_map/tij,tjf->tif/dot_general | solution.py:60
  60.4 2.1 %copy.11 = f32[6,256,256]{1,0,2:T(8,128)S(1)} copy(f32[6,256,256]{2,1,0:T(8,128)} %fusion.6) | data formatting | bytes 3145728 | tf_op jit(solution)/shard_map/tij,tjf->tif/dot_general | solution.py:60
  64.8 1.3 %collective-permute-start.22 = (f32[128,256]{1,0:T(8,128)S(1)}, f32[128,256]{1,0:T(8,128)S(1)}, u32[]{:S(2)}, u32[]{:S(2)}) collective-permute-start(f32[128,256]{1,0:T(8,128)S(1)} %get-tuple-element.6), channel_id=1, source_target_pairs={{0,24},{8,0},{16,8},{24,16},{1,25},{9,1},{17,9},{25,17},{2,26},{10... | collective-permute-start | bytes 393224 | tf_op jit(solution)/shard_map/ppermute | solution.py:23
  66.1 2.8 %collective-permute-done.20 = f32[128,256]{1,0:T(8,128)S(1)} collective-permute-done((f32[128,256]{1,0:T(8,128)S(1)}, f32[128,256]{1,0:T(8,128)S(1)}, u32[]{:S(2)}, u32[]{:S(2)}) %collective-permute-start.20) | collective-permute-done | bytes 131104 | tf_op jit(solution)/shard_map/ppermute | solution.py:23
  (72 shorter events, 16.0 us)
Async XLA Ops:
  0.0 29.9 %copy-start.1 = (bf16[1,1,6,256,256]{4,3,2,1,0:T(8,128)(2,1)S(1)}, bf16[1,1,6,256,256]{4,3,2,1,0:T(8,128)(2,1)}, u32[]{:S(2)}) copy-start(bf16[1,1,6,256,256]{4,3,2,1,0:T(8,128)(2,1)} %param.10) | copy-start | bytes 2359300
  3.0 5.3 %collective-permute-start = (f32[128]{0:T(128)S(1)}, f32[128]{0:T(128)S(1)}, u32[]{:S(2)}, u32[]{:S(2)}) collective-permute-start(f32[128]{0:T(128)S(1)} %get-tuple-element.13), channel_id=1, source_target_pairs={{0,8},{8,16},{16,24},{24,0},{1,9},{9,17},{17,25},{25,1},{2,10},{10... | collective-permute-start | bytes 1544 | tf_op jit(solution)/shard_map/ppermute | solution.py:23
  3.5 4.8 %collective-permute-start.1 = (f32[128]{0:T(128)S(1)}, f32[128]{0:T(128)S(1)}, u32[]{:S(2)}, u32[]{:S(2)}) collective-permute-start(f32[128]{0:T(128)S(1)} %get-tuple-element.15), channel_id=1, source_target_pairs={{0,16},{8,24},{16,0},{24,8},{1,17},{9,25},{17,1},{25,9},{2,18},{10... | collective-permute-start | bytes 1544 | tf_op jit(solution)/shard_map/ppermute | solution.py:23
  6.1 2.7 %collective-permute-start.2 = (f32[128]{0:T(128)S(1)}, f32[128]{0:T(128)S(1)}, u32[]{:S(2)}, u32[]{:S(2)}) collective-permute-start(f32[128]{0:T(128)S(1)} %get-tuple-element.14), channel_id=1, source_target_pairs={{0,24},{8,0},{16,8},{24,16},{1,25},{9,1},{17,9},{25,17},{2,26},{10... | collective-permute-start | bytes 1544 | tf_op jit(solution)/shard_map/ppermute | solution.py:23
  9.9 8.1 %collective-permute-start.3 = (bf16[128,256]{1,0:T(8,128)(2,1)S(1)}, bf16[128,256]{1,0:T(8,128)(2,1)S(1)}, u32[]{:S(2)}, u32[]{:S(2)}) collective-permute-start(bf16[128,256]{1,0:T(8,128)(2,1)S(1)} %get-tuple-element.17), channel_id=1, source_target_pairs={{0,7},{1,0},{2,1},{3,2},{4,3},{5,4},{6,5},{7,6},{8,15},{9,8},{10,9... | collective-permute-start | bytes 196616 | tf_op jit(solution)/shard_map/ppermute | solution.py:13
  14.4 5.3 %collective-permute-start.4 = (bf16[128,256]{1,0:T(8,128)(2,1)S(1)}, bf16[128,256]{1,0:T(8,128)(2,1)S(1)}, u32[]{:S(2)}, u32[]{:S(2)}) collective-permute-start(bf16[128,256]{1,0:T(8,128)(2,1)S(1)} %get-tuple-element.17), channel_id=1, source_target_pairs={{0,6},{1,7},{2,0},{3,1},{4,2},{5,3},{6,4},{7,5},{8,14},{9,15},{10,... | collective-permute-start | bytes 196616 | tf_op jit(solution)/shard_map/ppermute | solution.py:13
  14.9 6.0 %collective-permute-start.5 = (bf16[128,256]{1,0:T(8,128)(2,1)S(1)}, bf16[128,256]{1,0:T(8,128)(2,1)S(1)}, u32[]{:S(2)}, u32[]{:S(2)}) collective-permute-start(bf16[128,256]{1,0:T(8,128)(2,1)S(1)} %get-tuple-element.17), channel_id=1, source_target_pairs={{0,5},{1,6},{2,7},{3,0},{4,1},{5,2},{6,3},{7,4},{8,13},{9,14},{10,... | collective-permute-start | bytes 196616 | tf_op jit(solution)/shard_map/ppermute | solution.py:13
  14.9 12.0 %collective-permute-start.6 = (bf16[128,256]{1,0:T(8,128)(2,1)S(1)}, bf16[128,256]{1,0:T(8,128)(2,1)S(1)}, u32[]{:S(2)}, u32[]{:S(2)}) collective-permute-start(bf16[128,256]{1,0:T(8,128)(2,1)S(1)} %get-tuple-element.17), channel_id=1, source_target_pairs={{0,4},{1,5},{2,6},{3,7},{4,0},{5,1},{6,2},{7,3},{8,12},{9,13},{10,... | collective-permute-start | bytes 196616 | tf_op jit(solution)/shard_map/ppermute | solution.py:13
  17.9 11.3 %collective-permute-start.7 = (bf16[128,256]{1,0:T(8,128)(2,1)S(1)}, bf16[128,256]{1,0:T(8,128)(2,1)S(1)}, u32[]{:S(2)}, u32[]{:S(2)}) collective-permute-start(bf16[128,256]{1,0:T(8,128)(2,1)S(1)} %get-tuple-element.17), channel_id=1, source_target_pairs={{0,3},{1,4},{2,5},{3,6},{4,7},{5,0},{6,1},{7,2},{8,11},{9,12},{10,... | collective-permute-start | bytes 196616 | tf_op jit(solution)/shard_map/ppermute | solution.py:13
  17.9 11.3 %collective-permute-start.8 = (bf16[128,256]{1,0:T(8,128)(2,1)S(1)}, bf16[128,256]{1,0:T(8,128)(2,1)S(1)}, u32[]{:S(2)}, u32[]{:S(2)}) collective-permute-start(bf16[128,256]{1,0:T(8,128)(2,1)S(1)} %get-tuple-element.17), channel_id=1, source_target_pairs={{0,2},{1,3},{2,4},{3,5},{4,6},{5,7},{6,0},{7,1},{8,10},{9,11},{10,... | collective-permute-start | bytes 196616 | tf_op jit(solution)/shard_map/ppermute | solution.py:13
  19.7 9.5 %collective-permute-start.9 = (bf16[128,256]{1,0:T(8,128)(2,1)S(1)}, bf16[128,256]{1,0:T(8,128)(2,1)S(1)}, u32[]{:S(2)}, u32[]{:S(2)}) collective-permute-start(bf16[128,256]{1,0:T(8,128)(2,1)S(1)} %get-tuple-element.17), channel_id=1, source_target_pairs={{0,1},{1,2},{2,3},{3,4},{4,5},{5,6},{6,7},{7,0},{8,9},{9,10},{10,1... | collective-permute-start | bytes 196616 | tf_op jit(solution)/shard_map/ppermute | solution.py:13
  34.8 5.2 %collective-permute-start.10 = (f32[128,256]{1,0:T(8,128)S(1)}, f32[128,256]{1,0:T(8,128)S(1)}, u32[]{:S(2)}, u32[]{:S(2)}) collective-permute-start(f32[128,256]{1,0:T(8,128)S(1)} %get-tuple-element.8), channel_id=1, source_target_pairs={{0,8},{8,16},{16,24},{24,0},{1,9},{9,17},{17,25},{25,1},{2,10},{10... | collective-permute-start | bytes 393224 | tf_op jit(solution)/shard_map/ppermute | solution.py:23
  34.9 6.4 %collective-permute-start.11 = (f32[128,256]{1,0:T(8,128)S(1)}, f32[128,256]{1,0:T(8,128)S(1)}, u32[]{:S(2)}, u32[]{:S(2)}) collective-permute-start(f32[128,256]{1,0:T(8,128)S(1)} %get-tuple-element.10), channel_id=1, source_target_pairs={{0,16},{8,24},{16,0},{24,8},{1,17},{9,25},{17,1},{25,9},{2,18},{10... | collective-permute-start | bytes 393224 | tf_op jit(solution)/shard_map/ppermute | solution.py:23
  36.5 6.0 %collective-permute-start.12 = (f32[128,256]{1,0:T(8,128)S(1)}, f32[128,256]{1,0:T(8,128)S(1)}, u32[]{:S(2)}, u32[]{:S(2)}) collective-permute-start(f32[128,256]{1,0:T(8,128)S(1)} %get-tuple-element.9), channel_id=1, source_target_pairs={{0,24},{8,0},{16,8},{24,16},{1,25},{9,1},{17,9},{25,17},{2,26},{10... | collective-permute-start | bytes 393224 | tf_op jit(solution)/shard_map/ppermute | solution.py:23
  42.7 5.4 %collective-permute-start.13 = (bf16[128,256]{1,0:T(8,128)(2,1)S(1)}, bf16[128,256]{1,0:T(8,128)(2,1)S(1)}, u32[]{:S(2)}, u32[]{:S(2)}) collective-permute-start(bf16[128,256]{1,0:T(8,128)(2,1)S(1)} %get-tuple-element.19), channel_id=1, source_target_pairs={{0,7},{1,0},{2,1},{3,2},{4,3},{5,4},{6,5},{7,6},{8,15},{9,8},{10,9... | collective-permute-start | bytes 196616 | tf_op jit(solution)/shard_map/ppermute | solution.py:13
  42.8 6.7 %collective-permute-start.14 = (bf16[128,256]{1,0:T(8,128)(2,1)S(1)}, bf16[128,256]{1,0:T(8,128)(2,1)S(1)}, u32[]{:S(2)}, u32[]{:S(2)}) collective-permute-start(bf16[128,256]{1,0:T(8,128)(2,1)S(1)} %get-tuple-element.19), channel_id=1, source_target_pairs={{0,6},{1,7},{2,0},{3,1},{4,2},{5,3},{6,4},{7,5},{8,14},{9,15},{10,... | collective-permute-start | bytes 196616 | tf_op jit(solution)/shard_map/ppermute | solution.py:13
  44.1 7.5 %collective-permute-start.15 = (bf16[128,256]{1,0:T(8,128)(2,1)S(1)}, bf16[128,256]{1,0:T(8,128)(2,1)S(1)}, u32[]{:S(2)}, u32[]{:S(2)}) collective-permute-start(bf16[128,256]{1,0:T(8,128)(2,1)S(1)} %get-tuple-element.19), channel_id=1, source_target_pairs={{0,5},{1,6},{2,7},{3,0},{4,1},{5,2},{6,3},{7,4},{8,13},{9,14},{10,... | collective-permute-start | bytes 196616 | tf_op jit(solution)/shard_map/ppermute | solution.py:13
  45.0 11.7 %collective-permute-start.16 = (bf16[128,256]{1,0:T(8,128)(2,1)S(1)}, bf16[128,256]{1,0:T(8,128)(2,1)S(1)}, u32[]{:S(2)}, u32[]{:S(2)}) collective-permute-start(bf16[128,256]{1,0:T(8,128)(2,1)S(1)} %get-tuple-element.19), channel_id=1, source_target_pairs={{0,4},{1,5},{2,6},{3,7},{4,0},{5,1},{6,2},{7,3},{8,12},{9,13},{10,... | collective-permute-start | bytes 196616 | tf_op jit(solution)/shard_map/ppermute | solution.py:13
  47.2 10.9 %collective-permute-start.17 = (bf16[128,256]{1,0:T(8,128)(2,1)S(1)}, bf16[128,256]{1,0:T(8,128)(2,1)S(1)}, u32[]{:S(2)}, u32[]{:S(2)}) collective-permute-start(bf16[128,256]{1,0:T(8,128)(2,1)S(1)} %get-tuple-element.19), channel_id=1, source_target_pairs={{0,3},{1,4},{2,5},{3,6},{4,7},{5,0},{6,1},{7,2},{8,11},{9,12},{10,... | collective-permute-start | bytes 196616 | tf_op jit(solution)/shard_map/ppermute | solution.py:13
  48.2 10.0 %collective-permute-start.18 = (bf16[128,256]{1,0:T(8,128)(2,1)S(1)}, bf16[128,256]{1,0:T(8,128)(2,1)S(1)}, u32[]{:S(2)}, u32[]{:S(2)}) collective-permute-start(bf16[128,256]{1,0:T(8,128)(2,1)S(1)} %get-tuple-element.19), channel_id=1, source_target_pairs={{0,2},{1,3},{2,4},{3,5},{4,6},{5,7},{6,0},{7,1},{8,10},{9,11},{10,... | collective-permute-start | bytes 196616 | tf_op jit(solution)/shard_map/ppermute | solution.py:13
  49.5 8.7 %collective-permute-start.19 = (bf16[128,256]{1,0:T(8,128)(2,1)S(1)}, bf16[128,256]{1,0:T(8,128)(2,1)S(1)}, u32[]{:S(2)}, u32[]{:S(2)}) collective-permute-start(bf16[128,256]{1,0:T(8,128)(2,1)S(1)} %get-tuple-element.19), channel_id=1, source_target_pairs={{0,1},{1,2},{2,3},{3,4},{4,5},{5,6},{6,7},{7,0},{8,9},{9,10},{10,1... | collective-permute-start | bytes 196616 | tf_op jit(solution)/shard_map/ppermute | solution.py:13
  63.7 5.2 %collective-permute-start.20 = (f32[128,256]{1,0:T(8,128)S(1)}, f32[128,256]{1,0:T(8,128)S(1)}, u32[]{:S(2)}, u32[]{:S(2)}) collective-permute-start(f32[128,256]{1,0:T(8,128)S(1)} %get-tuple-element.5), channel_id=1, source_target_pairs={{0,8},{8,16},{16,24},{24,0},{1,9},{9,17},{17,25},{25,1},{2,10},{10... | collective-permute-start | bytes 393224 | tf_op jit(solution)/shard_map/ppermute | solution.py:23
  63.8 6.4 %collective-permute-start.21 = (f32[128,256]{1,0:T(8,128)S(1)}, f32[128,256]{1,0:T(8,128)S(1)}, u32[]{:S(2)}, u32[]{:S(2)}) collective-permute-start(f32[128,256]{1,0:T(8,128)S(1)} %get-tuple-element.7), channel_id=1, source_target_pairs={{0,16},{8,24},{16,0},{24,8},{1,17},{9,25},{17,1},{25,9},{2,18},{10... | collective-permute-start | bytes 393224 | tf_op jit(solution)/shard_map/ppermute | solution.py:23
  64.8 6.0 %collective-permute-start.22 = (f32[128,256]{1,0:T(8,128)S(1)}, f32[128,256]{1,0:T(8,128)S(1)}, u32[]{:S(2)}, u32[]{:S(2)}) collective-permute-start(f32[128,256]{1,0:T(8,128)S(1)} %get-tuple-element.6), channel_id=1, source_target_pairs={{0,24},{8,0},{16,8},{24,16},{1,25},{9,1},{17,9},{25,17},{2,26},{10... | collective-permute-start | bytes 393224 | tf_op jit(solution)/shard_map/ppermute | solution.py:23
  (4 other events, 24.0 us)

commit v2 on v1

--- a/solution.py
+++ b/solution.py
@@ -37,28 +37,40 @@
     width = features.shape[1]
     row_tiles = blk_size * node_dev // tile_size
     per_tile = tile_size // node_dev
+
+    group_features = gather_group(features, "grp", grp_size)
+
     live = lax.iota(jnp.int32, slots) < count_here
-    placing = (
-        (rows_here[None, :] == lax.iota(jnp.int32, row_tiles)[:, None]) & live[None, :]
-    ).astype(jnp.float32)
-    row_sums = jnp.sum(adjacency, axis=2, dtype=jnp.float32)
-    degree_part = jnp.dot(placing, row_sums, precision=lax.Precision.HIGHEST).reshape(
-        blk_size, node_dev
-    )
-    degree = scatter_sum(degree_part, "blk", blk_size)
-    scale = lax.rsqrt(1.0 + degree)[:, None]
+    placing = (rows_here[None, :] == lax.iota(jnp.int32, row_tiles)[:, None]) & live[None, :]
+    masked = jnp.where(placing[:, :, None, None], adjacency[None], jnp.zeros((), adjacency.dtype))
+    lhs = masked.transpose(0, 2, 1, 3).reshape(row_tiles * tile_size, slots * tile_size)
+    ones = jnp.ones((slots * tile_size, 128), adjacency.dtype)
+    row_sums = jnp.dot(lhs, ones, preferred_element_type=jnp.float32)[:, 0]
+    degree = scatter_sum(row_sums.reshape(blk_size, node_dev), "blk", blk_size)
+    norm = lax.rsqrt(1.0 + degree)
+    group_norm = gather_group(norm, "grp", grp_size)
+
     me_grp = lax.axis_index("grp")
     sources = cols_here[:, None] * per_tile + lax.iota(jnp.int32, per_tile)[None, :]
     slot_of_source = (sources - me_grp) % grp_size
+    scale = norm[:, None]
     hidden = features
     result = None
     for layer_index in range(LAYERS):
-        mixed = jnp.dot(hidden, weights[layer_index], preferred_element_type=jnp.float32)
-        scaled = (mixed * scale).astype(jnp.bfloat16)
-        received = gather_group(scaled, "grp", grp_size)
-        blocks = received[slot_of_source].reshape(slots, tile_size, width)
-        product = jnp.einsum("tij,tjf->tif", adjacency, blocks, preferred_element_type=jnp.float32)
-        placed = jnp.einsum("rt,tif->rif", placing, product, precision=lax.Precision.HIGHEST)
+        if layer_index == 0:
+            mixed = jnp.dot(
+                group_features.reshape(grp_size * node_dev, width),
+                weights[layer_index],
+                preferred_element_type=jnp.float32,
+            ).reshape(grp_size, node_dev, width)
+            received = (mixed * group_norm[:, :, None]).astype(jnp.bfloat16)
+            scaled = received[0]
+        else:
+            mixed = jnp.dot(hidden, weights[layer_index], preferred_element_type=jnp.float32)
+            scaled = (mixed * scale).astype(jnp.bfloat16)
+            received = gather_group(scaled, "grp", grp_size)
+        rhs = received[slot_of_source].reshape(slots * tile_size, width)
+        placed = jnp.dot(lhs, rhs, preferred_element_type=jnp.float32)
         partial_value = placed.reshape(blk_size, node_dev, width)
         summed = scatter_sum(partial_value, "blk", blk_size)
         pre = (summed + scaled.astype(jnp.float32)) * scale + biases[layer_index][None, :]

time: 72.7 us -> 79.2 us (1.089); the launches traced: 71.5 us -> 79 us
  starting transfers between devices: 29.7 us -> 37.8 us
  matrix products: 7.47 us -> 2.14 us
  local copies, waits for them, and re-layouts: 5.76 us -> 9.18 us
  waiting for transfers between devices: 24.7 us -> 26.2 us
    ppermute x14 -> x21, starting transfers between devices: 19.8 us -> 31.6 us  [gather_group(): received.append(lax.ppermute(block, axis, perm=perm))]
    dot_general x4 -> x0, local copies, waits for them, and re-layouts: 4.28 us -> none  [the longest x2 4.21 us: on_device(): jnp.einsum('tij,tjf->tif', adjacency, blocks, preferred_element_type=jnp....]
    dot_general x5 -> x4, matrix products: 6.19 us -> 1.93 us  [the longest x2 1.14 us: on_device(): placed = jnp.dot(lhs, rhs, preferred_element_type=jnp.float32)]
    ppermute x9, waiting for transfers between devices: 9.78 us -> 13.8 us  [scatter_sum(): total = total + lax.ppermute(outgoing, axis, perm=perm)]
    broadcast_in_dim x0 -> x4, local copies, waits for them, and re-layouts: none -> 3.71 us  [on_device(): jnp.where(placing[:, :, None, None], adjacency[None], jnp.zeros((), adjac...]
    ppermute x9, starting transfers between devices: 9.92 us -> 6.22 us  [scatter_sum(): total = total + lax.ppermute(outgoing, axis, perm=perm)]
    select_n x1 -> x2, local copies, waits for them, and re-layouts: 0.08 us -> 3.56 us  [the longest x1 3.48 us: on_device(): jnp.where(placing[:, :, None, None], adjacency[None], jnp.zeros((), adjac...]
    ppermute x14 -> x21, waiting for transfers between devices: 14.9 us -> 12.4 us  [gather_group(): received.append(lax.ppermute(block, axis, perm=perm))]
  transfers between devices with their start and end apart: 23 -> 30, of which waited for: 11 -> 11; matrix products, arithmetic and copies ran while one was open for 1% -> 5% of each run, Pallas kernels for 0% -> 0%
where the time goes in v2:
time: 79.2 us; the launch traced here: 79 us
  starting transfers between devices  37.8 us (48%)
  waiting for transfers between devices  26.2 us (33%)
  local copies, waits for them, and re-layouts  9.18 us (12%)
  other arithmetic  2.57 us (3%)
  matrix products  2.14 us (3%)
  between operations  1 us (1%)
    ppermute x21, starting transfers between devices, gather_group(): received.append(lax.ppermute(block, axis, perm=perm))  31.6 us
    ppermute x9, waiting for transfers between devices, scatter_sum(): total = total + lax.ppermute(outgoing, axis, perm=perm)  13.8 us
    ppermute x21, waiting for transfers between devices, gather_group(): received.append(lax.ppermute(block, axis, perm=perm))  12.4 us
    ppermute x9, starting transfers between devices, scatter_sum(): total = total + lax.ppermute(outgoing, axis, perm=perm)  6.22 us
    broadcast_in_dim x4, local copies, waits for them, and re-layouts, on_device(): jnp.where(placing[:, :, None, None], adjacency[None], jnp.zeros((), adjac...  3.71 us
    select_n x1, local copies, waits for them, and re-layouts, on_device(): jnp.where(placing[:, :, None, None], adjacency[None], jnp.zeros((), adjac...  3.48 us
    select_n x1, other arithmetic, on_device(): jnp.where(placing[:, :, None, None], adjacency[None], jnp.zeros((), adjac...  1.74 us
  transfers between devices with their start and end apart: 30, of which 11 were waited for; matrix products, arithmetic and copies ran while one was open for 5% of the time, Pallas kernels for 0%

profile of v2, /device:TPU:0, one launch (start us, length us, event | category | flops | bytes accessed | tf_op | source)
XLA Modules:
  0.0 79.0 jit_solution(12102389788144445242)
XLA Ops:
  0.7 1.6 %copy.9 = bf16[256,6,256]{2,1,0:T(8,128)(2,1)S(1)} copy(bf16[256,6,256]{2,0,1:T(8,128)(2,1)} %bitcast.145) | data formatting | bytes 1572864 | tf_op jit(solution)/shard_map/jit(_where)/broadcast_in_dim | solution.py:45
  2.6 1.8 %broadcast_in_dim.46 = pred[2,256,6,256]{3,2,1,0:T(8,128)(4,1)S(1)} reshape(pred[4,128,1536]{2,1,0:T(8,128)(4,1)S(1)} %broadcast_in_dim.45) | data formatting | bytes 1572864 | tf_op jit(solution)/shard_map/jit(_where)/broadcast_in_dim | solution.py:45
  4.4 1.7 %broadcast_select_fusion = (bf16[2,256,6,256]{3,2,1,0:T(8,128)(2,1)S(1)}, bf16[2,256,6,256]{3,2,1,0:T(8,128)(2,1)}) fusion(pred[2,6]{1,0:T(4,128)(4,1)S(1)} %compare_and_fusion, bf16[256,6,256]{2,1,0:T(8,128)(2,1)S(1)} %copy.9, pred[2,256,6,256]{3,2,1,0:T(8,128)(4,1)S(1)} %broadcast_in_dim.46), kind=kLoop, calls=%fused_computation.2 | loop fusion | flops 1572864 | bytes 4718604 | tf_op jit(solution)/shard_map/jit(_where)/select_n | solution.py:45
  7.2 2.5 %collective-permute-start.9 = (f32[128]{0:T(128)S(1)}, f32[128]{0:T(128)S(1)}, u32[]{:S(2)}, u32[]{:S(2)}) collective-permute-start(f32[128]{0:T(128)S(1)} %get-tuple-element.16), channel_id=1, source_target_pairs={{0,24},{8,0},{16,8},{24,16},{1,25},{9,1},{17,9},{25,17},{2,26},{10... | collective-permute-start | bytes 1544 | tf_op jit(solution)/shard_map/ppermute | solution.py:23
  10.5 4.5 %collective-permute-start = (bf16[128,256]{1,0:T(8,128)(2,1)S(1)}, bf16[128,256]{1,0:T(8,128)(2,1)S(1)}, u32[]{:S(2)}, u32[]{:S(2)}) collective-permute-start(bf16[128,256]{1,0:T(8,128)(2,1)S(1)} %copy-done.1), channel_id=1, source_target_pairs={{0,7},{1,0},{2,1},{3,2},{4,3},{5,4},{6,5},{7,6},{8,15},{9,8},{10,9... | collective-permute-start | bytes 196616 | tf_op jit(solution)/shard_map/ppermute | solution.py:13
  15.1 2.8 %collective-permute-start.10 = (f32[128]{0:T(128)S(1)}, f32[128]{0:T(128)S(1)}, u32[]{:S(2)}, u32[]{:S(2)}) collective-permute-start(f32[128]{0:T(128)S(1)} %add_rsqrt_fusion), channel_id=1, source_target_pairs={{0,7},{1,0},{2,1},{3,2},{4,3},{5,4},{6,5},{7,6},{8,15},{9,8},{10,9... | collective-permute-start | bytes 1544 | tf_op jit(solution)/shard_map/ppermute | solution.py:13
  18.5 3.0 %collective-permute-start.13 = (f32[128]{0:T(128)S(1)}, f32[128]{0:T(128)S(1)}, u32[]{:S(2)}, u32[]{:S(2)}) collective-permute-start(f32[128]{0:T(128)S(1)} %add_rsqrt_fusion), channel_id=1, source_target_pairs={{0,4},{1,5},{2,6},{3,7},{4,0},{5,1},{6,2},{7,3},{8,12},{9,13},{10,... | collective-permute-start | bytes 1544 | tf_op jit(solution)/shard_map/ppermute | solution.py:13
  21.5 1.8 %collective-permute-start.15 = (f32[128]{0:T(128)S(1)}, f32[128]{0:T(128)S(1)}, u32[]{:S(2)}, u32[]{:S(2)}) collective-permute-start(f32[128]{0:T(128)S(1)} %add_rsqrt_fusion), channel_id=1, source_target_pairs={{0,2},{1,3},{2,4},{3,5},{4,6},{5,7},{6,0},{7,1},{8,10},{9,11},{10,... | collective-permute-start | bytes 1544 | tf_op jit(solution)/shard_map/ppermute | solution.py:13
  24.5 3.5 %reshape.196 = bf16[4,128,1536]{2,1,0:T(8,128)(2,1)S(1)} reshape(bf16[2,256,6,256]{3,2,1,0:T(8,128)(2,1)} %get-tuple-element.6) | data formatting | bytes 3145728 | tf_op jit(solution)/shard_map/jit(_where)/select_n | solution.py:45
  28.0 2.5 %collective-permute-start.1 = (bf16[128,256]{1,0:T(8,128)(2,1)S(1)}, bf16[128,256]{1,0:T(8,128)(2,1)S(1)}, u32[]{:S(2)}, u32[]{:S(2)}) collective-permute-start(bf16[128,256]{1,0:T(8,128)(2,1)S(1)} %copy-done.1), channel_id=1, source_target_pairs={{0,6},{1,7},{2,0},{3,1},{4,2},{5,3},{6,4},{7,5},{8,14},{9,15},{10,... | collective-permute-start | bytes 196616 | tf_op jit(solution)/shard_map/ppermute | solution.py:13
  30.4 2.9 %collective-permute-start.2 = (bf16[128,256]{1,0:T(8,128)(2,1)S(1)}, bf16[128,256]{1,0:T(8,128)(2,1)S(1)}, u32[]{:S(2)}, u32[]{:S(2)}) collective-permute-start(bf16[128,256]{1,0:T(8,128)(2,1)S(1)} %copy-done.1), channel_id=1, source_target_pairs={{0,5},{1,6},{2,7},{3,0},{4,1},{5,2},{6,3},{7,4},{8,13},{9,14},{10,... | collective-permute-start | bytes 196616 | tf_op jit(solution)/shard_map/ppermute | solution.py:13
  34.6 1.8 %collective-permute-start.5 = (bf16[128,256]{1,0:T(8,128)(2,1)S(1)}, bf16[128,256]{1,0:T(8,128)(2,1)S(1)}, u32[]{:S(2)}, u32[]{:S(2)}) collective-permute-start(bf16[128,256]{1,0:T(8,128)(2,1)S(1)} %copy-done.1), channel_id=1, source_target_pairs={{0,2},{1,3},{2,4},{3,5},{4,6},{5,7},{6,0},{7,1},{8,10},{9,11},{10,... | collective-permute-start | bytes 196616 | tf_op jit(solution)/shard_map/ppermute | solution.py:13
  36.4 1.6 %collective-permute-start.6 = (bf16[128,256]{1,0:T(8,128)(2,1)S(1)}, bf16[128,256]{1,0:T(8,128)(2,1)S(1)}, u32[]{:S(2)}, u32[]{:S(2)}) collective-permute-start(bf16[128,256]{1,0:T(8,128)(2,1)S(1)} %copy-done.1), channel_id=1, source_target_pairs={{0,1},{1,2},{2,3},{3,4},{4,5},{5,6},{6,7},{7,0},{8,9},{9,10},{10,1... | collective-permute-start | bytes 196616 | tf_op jit(solution)/shard_map/ppermute | solution.py:13
  37.9 3.3 %collective-permute-done.3 = bf16[128,256]{1,0:T(8,128)(2,1)S(1)} collective-permute-done((bf16[128,256]{1,0:T(8,128)(2,1)S(1)}, bf16[128,256]{1,0:T(8,128)(2,1)S(1)}, u32[]{:S(2)}, u32[]{:S(2)}) %collective-permute-start.3) | collective-permute-done | bytes 65568 | tf_op jit(solution)/shard_map/ppermute | solution.py:13
  42.3 1.7 %collective-permute-done.6 = bf16[128,256]{1,0:T(8,128)(2,1)S(1)} collective-permute-done((bf16[128,256]{1,0:T(8,128)(2,1)S(1)}, bf16[128,256]{1,0:T(8,128)(2,1)S(1)}, u32[]{:S(2)}, u32[]{:S(2)}) %collective-permute-start.6) | collective-permute-done | bytes 65568 | tf_op jit(solution)/shard_map/ppermute | solution.py:13
  45.6 1.5 %collective-permute-start.18 = (f32[128,256]{1,0:T(8,128)S(1)}, f32[128,256]{1,0:T(8,128)S(1)}, u32[]{:S(2)}, u32[]{:S(2)}) collective-permute-start(f32[128,256]{1,0:T(8,128)S(1)} %get-tuple-element.12), channel_id=1, source_target_pairs={{0,16},{8,24},{16,0},{24,8},{1,17},{9,25},{17,1},{25,9},{2,18},{10... | collective-permute-start | bytes 393224 | tf_op jit(solution)/shard_map/ppermute | solution.py:23
  48.6 5.4 %collective-permute-done.18 = f32[128,256]{1,0:T(8,128)S(1)} collective-permute-done((f32[128,256]{1,0:T(8,128)S(1)}, f32[128,256]{1,0:T(8,128)S(1)}, u32[]{:S(2)}, u32[]{:S(2)}) %collective-permute-start.18) | collective-permute-done | bytes 131104 | tf_op jit(solution)/shard_map/ppermute | solution.py:23
  54.4 1.4 %collective-permute-start.20 = (bf16[128,256]{1,0:T(8,128)(2,1)S(1)}, bf16[128,256]{1,0:T(8,128)(2,1)S(1)}, u32[]{:S(2)}, u32[]{:S(2)}) collective-permute-start(bf16[128,256]{1,0:T(8,128)(2,1)S(1)} %get-tuple-element.19), channel_id=1, source_target_pairs={{0,7},{1,0},{2,1},{3,2},{4,3},{5,4},{6,5},{7,6},{8,15},{9,8},{10,9... | collective-permute-start | bytes 196616 | tf_op jit(solution)/shard_map/ppermute | solution.py:13
  56.2 2.6 %collective-permute-start.23 = (bf16[128,256]{1,0:T(8,128)(2,1)S(1)}, bf16[128,256]{1,0:T(8,128)(2,1)S(1)}, u32[]{:S(2)}, u32[]{:S(2)}) collective-permute-start(bf16[128,256]{1,0:T(8,128)(2,1)S(1)} %get-tuple-element.19), channel_id=1, source_target_pairs={{0,4},{1,5},{2,6},{3,7},{4,0},{5,1},{6,2},{7,3},{8,12},{9,13},{10,... | collective-permute-start | bytes 196616 | tf_op jit(solution)/shard_map/ppermute | solution.py:13
  58.8 1.3 %collective-permute-start.24 = (bf16[128,256]{1,0:T(8,128)(2,1)S(1)}, bf16[128,256]{1,0:T(8,128)(2,1)S(1)}, u32[]{:S(2)}, u32[]{:S(2)}) collective-permute-start(bf16[128,256]{1,0:T(8,128)(2,1)S(1)} %get-tuple-element.19), channel_id=1, source_target_pairs={{0,3},{1,4},{2,5},{3,6},{4,7},{5,0},{6,1},{7,2},{8,11},{9,12},{10,... | collective-permute-start | bytes 196616 | tf_op jit(solution)/shard_map/ppermute | solution.py:13
  62.4 2.8 %collective-permute-done.23 = bf16[128,256]{1,0:T(8,128)(2,1)S(1)} collective-permute-done((bf16[128,256]{1,0:T(8,128)(2,1)S(1)}, bf16[128,256]{1,0:T(8,128)(2,1)S(1)}, u32[]{:S(2)}, u32[]{:S(2)}) %collective-permute-start.23) | collective-permute-done | bytes 65568 | tf_op jit(solution)/shard_map/ppermute | solution.py:13
  65.2 3.5 %collective-permute-done.24 = bf16[128,256]{1,0:T(8,128)(2,1)S(1)} collective-permute-done((bf16[128,256]{1,0:T(8,128)(2,1)S(1)}, bf16[128,256]{1,0:T(8,128)(2,1)S(1)}, u32[]{:S(2)}, u32[]{:S(2)}) %collective-permute-start.24) | collective-permute-done | bytes 65568 | tf_op jit(solution)/shard_map/ppermute | solution.py:13
  71.3 2.2 %collective-permute-done.29 = f32[128,256]{1,0:T(8,128)S(1)} collective-permute-done((f32[128,256]{1,0:T(8,128)S(1)}, f32[128,256]{1,0:T(8,128)S(1)}, u32[]{:S(2)}, u32[]{:S(2)}) %collective-permute-start.29) | collective-permute-done | bytes 131104 | tf_op jit(solution)/shard_map/ppermute | solution.py:23
  73.5 4.2 %collective-permute-done.28 = f32[128,256]{1,0:T(8,128)S(1)} collective-permute-done((f32[128,256]{1,0:T(8,128)S(1)}, f32[128,256]{1,0:T(8,128)S(1)}, u32[]{:S(2)}, u32[]{:S(2)}) %collective-permute-start.28) | collective-permute-done | bytes 131104 | tf_op jit(solution)/shard_map/ppermute | solution.py:23
  (89 shorter events, 16.0 us)
Async XLA Ops:
  7.2 7.8 %collective-permute-start.9 = (f32[128]{0:T(128)S(1)}, f32[128]{0:T(128)S(1)}, u32[]{:S(2)}, u32[]{:S(2)}) collective-permute-start(f32[128]{0:T(128)S(1)} %get-tuple-element.16), channel_id=1, source_target_pairs={{0,24},{8,0},{16,8},{24,16},{1,25},{9,1},{17,9},{25,17},{2,26},{10... | collective-permute-start | bytes 1544 | tf_op jit(solution)/shard_map/ppermute | solution.py:23
  9.7 5.4 %collective-permute-start.8 = (f32[128]{0:T(128)S(1)}, f32[128]{0:T(128)S(1)}, u32[]{:S(2)}, u32[]{:S(2)}) collective-permute-start(f32[128]{0:T(128)S(1)} %get-tuple-element.17), channel_id=1, source_target_pairs={{0,16},{8,24},{16,0},{24,8},{1,17},{9,25},{17,1},{25,9},{2,18},{10... | collective-permute-start | bytes 1544 | tf_op jit(solution)/shard_map/ppermute | solution.py:23
  10.5 24.1 %collective-permute-start = (bf16[128,256]{1,0:T(8,128)(2,1)S(1)}, bf16[128,256]{1,0:T(8,128)(2,1)S(1)}, u32[]{:S(2)}, u32[]{:S(2)}) collective-permute-start(bf16[128,256]{1,0:T(8,128)(2,1)S(1)} %copy-done.1), channel_id=1, source_target_pairs={{0,7},{1,0},{2,1},{3,2},{4,3},{5,4},{6,5},{7,6},{8,15},{9,8},{10,9... | collective-permute-start | bytes 196616 | tf_op jit(solution)/shard_map/ppermute | solution.py:13
  15.1 6.4 %collective-permute-start.10 = (f32[128]{0:T(128)S(1)}, f32[128]{0:T(128)S(1)}, u32[]{:S(2)}, u32[]{:S(2)}) collective-permute-start(f32[128]{0:T(128)S(1)} %add_rsqrt_fusion), channel_id=1, source_target_pairs={{0,7},{1,0},{2,1},{3,2},{4,3},{5,4},{6,5},{7,6},{8,15},{9,8},{10,9... | collective-permute-start | bytes 1544 | tf_op jit(solution)/shard_map/ppermute | solution.py:13
  18.5 9.5 %collective-permute-start.13 = (f32[128]{0:T(128)S(1)}, f32[128]{0:T(128)S(1)}, u32[]{:S(2)}, u32[]{:S(2)}) collective-permute-start(f32[128]{0:T(128)S(1)} %add_rsqrt_fusion), channel_id=1, source_target_pairs={{0,4},{1,5},{2,6},{3,7},{4,0},{5,1},{6,2},{7,3},{8,12},{9,13},{10,... | collective-permute-start | bytes 1544 | tf_op jit(solution)/shard_map/ppermute | solution.py:13
  21.5 8.9 %collective-permute-start.14 = (f32[128]{0:T(128)S(1)}, f32[128]{0:T(128)S(1)}, u32[]{:S(2)}, u32[]{:S(2)}) collective-permute-start(f32[128]{0:T(128)S(1)} %add_rsqrt_fusion), channel_id=1, source_target_pairs={{0,3},{1,4},{2,5},{3,6},{4,7},{5,0},{6,1},{7,2},{8,11},{9,12},{10,... | collective-permute-start | bytes 1544 | tf_op jit(solution)/shard_map/ppermute | solution.py:13
  21.5 11.8 %collective-permute-start.15 = (f32[128]{0:T(128)S(1)}, f32[128]{0:T(128)S(1)}, u32[]{:S(2)}, u32[]{:S(2)}) collective-permute-start(f32[128]{0:T(128)S(1)} %add_rsqrt_fusion), channel_id=1, source_target_pairs={{0,2},{1,3},{2,4},{3,5},{4,6},{5,7},{6,0},{7,1},{8,10},{9,11},{10,... | collective-permute-start | bytes 1544 | tf_op jit(solution)/shard_map/ppermute | solution.py:13
  23.3 11.2 %collective-permute-start.16 = (f32[128]{0:T(128)S(1)}, f32[128]{0:T(128)S(1)}, u32[]{:S(2)}, u32[]{:S(2)}) collective-permute-start(f32[128]{0:T(128)S(1)} %add_rsqrt_fusion), channel_id=1, source_target_pairs={{0,1},{1,2},{2,3},{3,4},{4,5},{5,6},{6,7},{7,0},{8,9},{9,10},{10,1... | collective-permute-start | bytes 1544 | tf_op jit(solution)/shard_map/ppermute | solution.py:13
  28.0 8.4 %collective-permute-start.1 = (bf16[128,256]{1,0:T(8,128)(2,1)S(1)}, bf16[128,256]{1,0:T(8,128)(2,1)S(1)}, u32[]{:S(2)}, u32[]{:S(2)}) collective-permute-start(bf16[128,256]{1,0:T(8,128)(2,1)S(1)} %copy-done.1), channel_id=1, source_target_pairs={{0,6},{1,7},{2,0},{3,1},{4,2},{5,3},{6,4},{7,5},{8,14},{9,15},{10,... | collective-permute-start | bytes 196616 | tf_op jit(solution)/shard_map/ppermute | solution.py:13
  30.4 7.5 %collective-permute-start.2 = (bf16[128,256]{1,0:T(8,128)(2,1)S(1)}, bf16[128,256]{1,0:T(8,128)(2,1)S(1)}, u32[]{:S(2)}, u32[]{:S(2)}) collective-permute-start(bf16[128,256]{1,0:T(8,128)(2,1)S(1)} %copy-done.1), channel_id=1, source_target_pairs={{0,5},{1,6},{2,7},{3,0},{4,1},{5,2},{6,3},{7,4},{8,13},{9,14},{10,... | collective-permute-start | bytes 196616 | tf_op jit(solution)/shard_map/ppermute | solution.py:13
  33.3 8.0 %collective-permute-start.3 = (bf16[128,256]{1,0:T(8,128)(2,1)S(1)}, bf16[128,256]{1,0:T(8,128)(2,1)S(1)}, u32[]{:S(2)}, u32[]{:S(2)}) collective-permute-start(bf16[128,256]{1,0:T(8,128)(2,1)S(1)} %copy-done.1), channel_id=1, source_target_pairs={{0,4},{1,5},{2,6},{3,7},{4,0},{5,1},{6,2},{7,3},{8,12},{9,13},{10,... | collective-permute-start | bytes 196616 | tf_op jit(solution)/shard_map/ppermute | solution.py:13
  34.6 7.7 %collective-permute-start.4 = (bf16[128,256]{1,0:T(8,128)(2,1)S(1)}, bf16[128,256]{1,0:T(8,128)(2,1)S(1)}, u32[]{:S(2)}, u32[]{:S(2)}) collective-permute-start(bf16[128,256]{1,0:T(8,128)(2,1)S(1)} %copy-done.1), channel_id=1, source_target_pairs={{0,3},{1,4},{2,5},{3,6},{4,7},{5,0},{6,1},{7,2},{8,11},{9,12},{10,... | collective-permute-start | bytes 196616 | tf_op jit(solution)/shard_map/ppermute | solution.py:13
  34.6 7.7 %collective-permute-start.5 = (bf16[128,256]{1,0:T(8,128)(2,1)S(1)}, bf16[128,256]{1,0:T(8,128)(2,1)S(1)}, u32[]{:S(2)}, u32[]{:S(2)}) collective-permute-start(bf16[128,256]{1,0:T(8,128)(2,1)S(1)} %copy-done.1), channel_id=1, source_target_pairs={{0,2},{1,3},{2,4},{3,5},{4,6},{5,7},{6,0},{7,1},{8,10},{9,11},{10,... | collective-permute-start | bytes 196616 | tf_op jit(solution)/shard_map/ppermute | solution.py:13
  36.4 7.6 %collective-permute-start.6 = (bf16[128,256]{1,0:T(8,128)(2,1)S(1)}, bf16[128,256]{1,0:T(8,128)(2,1)S(1)}, u32[]{:S(2)}, u32[]{:S(2)}) collective-permute-start(bf16[128,256]{1,0:T(8,128)(2,1)S(1)} %copy-done.1), channel_id=1, source_target_pairs={{0,1},{1,2},{2,3},{3,4},{4,5},{5,6},{6,7},{7,0},{8,9},{9,10},{10,1... | collective-permute-start | bytes 196616 | tf_op jit(solution)/shard_map/ppermute | solution.py:13
  45.6 8.3 %collective-permute-start.18 = (f32[128,256]{1,0:T(8,128)S(1)}, f32[128,256]{1,0:T(8,128)S(1)}, u32[]{:S(2)}, u32[]{:S(2)}) collective-permute-start(f32[128,256]{1,0:T(8,128)S(1)} %get-tuple-element.12), channel_id=1, source_target_pairs={{0,16},{8,24},{16,0},{24,8},{1,17},{9,25},{17,1},{25,9},{2,18},{10... | collective-permute-start | bytes 393224 | tf_op jit(solution)/shard_map/ppermute | solution.py:23
  47.1 7.1 %collective-permute-start.17 = (f32[128,256]{1,0:T(8,128)S(1)}, f32[128,256]{1,0:T(8,128)S(1)}, u32[]{:S(2)}, u32[]{:S(2)}) collective-permute-start(f32[128,256]{1,0:T(8,128)S(1)} %get-tuple-element.10), channel_id=1, source_target_pairs={{0,8},{8,16},{16,24},{24,0},{1,9},{9,17},{17,25},{25,1},{2,10},{10... | collective-permute-start | bytes 393224 | tf_op jit(solution)/shard_map/ppermute | solution.py:23
  54.4 5.8 %collective-permute-start.20 = (bf16[128,256]{1,0:T(8,128)(2,1)S(1)}, bf16[128,256]{1,0:T(8,128)(2,1)S(1)}, u32[]{:S(2)}, u32[]{:S(2)}) collective-permute-start(bf16[128,256]{1,0:T(8,128)(2,1)S(1)} %get-tuple-element.19), channel_id=1, source_target_pairs={{0,7},{1,0},{2,1},{3,2},{4,3},{5,4},{6,5},{7,6},{8,15},{9,8},{10,9... | collective-permute-start | bytes 196616 | tf_op jit(solution)/shard_map/ppermute | solution.py:13
  55.8 6.6 %collective-permute-start.22 = (bf16[128,256]{1,0:T(8,128)(2,1)S(1)}, bf16[128,256]{1,0:T(8,128)(2,1)S(1)}, u32[]{:S(2)}, u32[]{:S(2)}) collective-permute-start(bf16[128,256]{1,0:T(8,128)(2,1)S(1)} %get-tuple-element.19), channel_id=1, source_target_pairs={{0,5},{1,6},{2,7},{3,0},{4,1},{5,2},{6,3},{7,4},{8,13},{9,14},{10,... | collective-permute-start | bytes 196616 | tf_op jit(solution)/shard_map/ppermute | solution.py:13
  56.2 9.0 %collective-permute-start.23 = (bf16[128,256]{1,0:T(8,128)(2,1)S(1)}, bf16[128,256]{1,0:T(8,128)(2,1)S(1)}, u32[]{:S(2)}, u32[]{:S(2)}) collective-permute-start(bf16[128,256]{1,0:T(8,128)(2,1)S(1)} %get-tuple-element.19), channel_id=1, source_target_pairs={{0,4},{1,5},{2,6},{3,7},{4,0},{5,1},{6,2},{7,3},{8,12},{9,13},{10,... | collective-permute-start | bytes 196616 | tf_op jit(solution)/shard_map/ppermute | solution.py:13
  58.8 9.9 %collective-permute-start.24 = (bf16[128,256]{1,0:T(8,128)(2,1)S(1)}, bf16[128,256]{1,0:T(8,128)(2,1)S(1)}, u32[]{:S(2)}, u32[]{:S(2)}) collective-permute-start(bf16[128,256]{1,0:T(8,128)(2,1)S(1)} %get-tuple-element.19), channel_id=1, source_target_pairs={{0,3},{1,4},{2,5},{3,6},{4,7},{5,0},{6,1},{7,2},{8,11},{9,12},{10,... | collective-permute-start | bytes 196616 | tf_op jit(solution)/shard_map/ppermute | solution.py:13
  60.2 8.6 %collective-permute-start.25 = (bf16[128,256]{1,0:T(8,128)(2,1)S(1)}, bf16[128,256]{1,0:T(8,128)(2,1)S(1)}, u32[]{:S(2)}, u32[]{:S(2)}) collective-permute-start(bf16[128,256]{1,0:T(8,128)(2,1)S(1)} %get-tuple-element.19), channel_id=1, source_target_pairs={{0,2},{1,3},{2,4},{3,5},{4,6},{5,7},{6,0},{7,1},{8,10},{9,11},{10,... | collective-permute-start | bytes 196616 | tf_op jit(solution)/shard_map/ppermute | solution.py:13
  61.1 7.7 %collective-permute-start.26 = (bf16[128,256]{1,0:T(8,128)(2,1)S(1)}, bf16[128,256]{1,0:T(8,128)(2,1)S(1)}, u32[]{:S(2)}, u32[]{:S(2)}) collective-permute-start(bf16[128,256]{1,0:T(8,128)(2,1)S(1)} %get-tuple-element.19), channel_id=1, source_target_pairs={{0,1},{1,2},{2,3},{3,4},{4,5},{5,6},{6,7},{7,0},{8,9},{9,10},{10,1... | collective-permute-start | bytes 196616 | tf_op jit(solution)/shard_map/ppermute | solution.py:13
  70.1 7.6 %collective-permute-start.28 = (f32[128,256]{1,0:T(8,128)S(1)}, f32[128,256]{1,0:T(8,128)S(1)}, u32[]{:S(2)}, u32[]{:S(2)}) collective-permute-start(f32[128,256]{1,0:T(8,128)S(1)} %get-tuple-element.9), channel_id=1, source_target_pairs={{0,16},{8,24},{16,0},{24,8},{1,17},{9,25},{17,1},{25,9},{2,18},{10... | collective-permute-start | bytes 393224 | tf_op jit(solution)/shard_map/ppermute | solution.py:23
  71.2 7.1 %collective-permute-start.27 = (f32[128,256]{1,0:T(8,128)S(1)}, f32[128,256]{1,0:T(8,128)S(1)}, u32[]{:S(2)}, u32[]{:S(2)}) collective-permute-start(f32[128,256]{1,0:T(8,128)S(1)} %get-tuple-element.7), channel_id=1, source_target_pairs={{0,8},{8,16},{16,24},{24,0},{1,9},{9,17},{17,25},{25,1},{2,10},{10... | collective-permute-start | bytes 393224 | tf_op jit(solution)/shard_map/ppermute | solution.py:23
  (11 other events, 61.5 us)

commit v3 on v1

v3 whole, which is shorter than its diff:
```python
import jax
import jax.numpy as jnp
from jax import lax
from jax.sharding import PartitionSpec as P

LAYERS = 2
TWO_STAGE_GATHER = False


def gather_group(block, axis, size):
    received = [block]
    for shift in range(1, size):
        perm = [(i, (i - shift) % size) for i in range(size)]
        received.append(lax.ppermute(block, axis, perm=perm))
    return jnp.stack(received)


def gather_tiles(block, axis, size, per_tile):
    me = lax.axis_index(axis)
    pos = me % per_tile
    parts = [block]
    for shift in range(1, per_tile):
        perm = [(i, i - i % per_tile + (i + shift) % per_tile) for i in range(size)]
        parts.append(lax.ppermute(block, axis, perm=perm))
    stacked = jnp.stack(parts)
    order = (lax.iota(jnp.int32, per_tile) - pos) % per_tile
    tile = stacked[order]
    tiles = [tile]
    n_tiles = size // per_tile
    for shift in range(1, n_tiles):
        perm = [(i, (i - shift * per_tile) % size) for i in range(size)]
        tiles.append(lax.ppermute(tile, axis, perm=perm))
    return jnp.stack(tiles)


def scatter_sum(parts, axis, size):
    me = lax.axis_index(axis)
    total = lax.dynamic_index_in_dim(parts, me, 0, keepdims=False)
    for shift in range(1, size):
        perm = [(i, (i + shift) % size) for i in range(size)]
        outgoing = lax.dynamic_index_in_dim(parts, (me + shift) % size, 0, keepdims=False)
        total = total + lax.ppermute(outgoing, axis, perm=perm)
    return total


def scatter_sum_pairs(parts, axis, size):
    if size % 2:
        return scatter_sum(parts, axis, size)
    me = lax.axis_index(axis)
    low = me % 2
    by_pair = parts.reshape((size // 2, 2) + parts.shape[1:])
    mine = lax.dynamic_index_in_dim(by_pair, low, 1, keepdims=False)
    theirs = lax.dynamic_index_in_dim(by_pair, 1 - low, 1, keepdims=False)
    perm = [(i, i ^ 1) for i in range(size)]
    half = mine + lax.ppermute(theirs, axis, perm=perm)
    pair_me = me // 2
    total = lax.dynamic_index_in_dim(half, pair_me, 0, keepdims=False)
    for shift in range(1, size // 2):
        perm = [(i, (i + 2 * shift) % size) for i in range(size)]
        outgoing = lax.dynamic_index_in_dim(half, (pair_me + shift) % (size // 2), 0, keepdims=False)
        total = total + lax.ppermute(outgoing, axis, perm=perm)
    return total


def on_device(features, weights, biases, adjacency, tile_row, tile_column, tile_count):
    adjacency = adjacency[0, 0]
    rows_here = tile_row[0, 0]
    cols_here = tile_column[0, 0]
    count_here = tile_count[0, 0]
    blk_size = lax.axis_size("blk")
    grp_size = lax.axis_size("grp")
    node_dev = features.shape[0]
    tile_size = adjacency.shape[1]
    slots = adjacency.shape[0]
    width = features.shape[1]
    row_tiles = blk_size * node_dev // tile_size
    per_tile = tile_size // node_dev
    live = lax.iota(jnp.int32, slots) < count_here
    placing = (rows_here[:, None] == lax.iota(jnp.int32, row_tiles)[None, :]) & live[:, None]
    lhs = adjacency.transpose(1, 0, 2).reshape(tile_size, slots * tile_size)
    pick = jnp.broadcast_to(placing[:, None, :, None], (slots, tile_size, row_tiles, 128))
    row_sums = jnp.dot(
        lhs, pick.astype(adjacency.dtype).reshape(slots * tile_size, row_tiles * 128),
        preferred_element_type=jnp.float32,
    )
    degree_part = row_sums.reshape(tile_size, row_tiles, 128)[:, :, 0].T.reshape(blk_size, node_dev)
    degree = scatter_sum_pairs(degree_part, "blk", blk_size)
    scale = lax.rsqrt(1.0 + degree)[:, None]
    me_grp = lax.axis_index("grp")
    hidden = features
    result = None
    for layer_index in range(LAYERS):
        mixed = jnp.dot(hidden, weights[layer_index], preferred_element_type=jnp.float32)
        scaled = (mixed * scale).astype(jnp.bfloat16)
        if TWO_STAGE_GATHER and per_tile > 1 and grp_size % per_tile == 0:
            tiles = gather_tiles(scaled, "grp", grp_size, per_tile)
            n_tiles = grp_size // per_tile
            blocks = tiles[(cols_here - me_grp // per_tile) % n_tiles].reshape(slots, tile_size, width)
        else:
            received = gather_group(scaled, "grp", grp_size)
            sources = cols_here[:, None] * per_tile + lax.iota(jnp.int32, per_tile)[None, :]
            blocks = received[(sources - me_grp) % grp_size].reshape(slots, tile_size, width)
        rhs = jnp.where(
            placing[:, None, :, None], blocks[:, :, None, :], jnp.zeros((), blocks.dtype)
        ).reshape(slots * tile_size, row_tiles * width)
        out = jnp.dot(lhs, rhs, preferred_element_type=jnp.float32)
        partial_value = (
            out.reshape(per_tile, node_dev, row_tiles, width).transpose(2, 0, 1, 3)
            .reshape(blk_size, node_dev, width)
        )
        summed = scatter_sum_pairs(partial_value, "blk", blk_size)
        pre = (summed + scaled.astype(jnp.float32)) * scale + biases[layer_index][None, :]
        if layer_index < LAYERS - 1:
            hidden = jnp.maximum(pre, 0.0).astype(jnp.bfloat16)
        else:
            result = pre.astype(jnp.bfloat16)
    return result


def solution(mesh):
    placed = (
        P(("blk", "grp"), None),
        P(),
        P(),
        P("blk", "grp", None, None, None),
        P("blk", "grp", None),
        P("blk", "grp", None),
        P("blk", "grp"),
    )
    return jax.shard_map(
        on_device, mesh=mesh, in_specs=placed, out_specs=P(("blk", "grp"), None), check_vma=False
    )
```

time: 72.7 us -> 66.3 us (0.912); the launches traced: 71.5 us -> 66.1 us
  matrix products: 7.47 us -> 1.97 us
  starting transfers between devices: 29.7 us -> 27.4 us
  other arithmetic: 2.89 us -> 4.21 us
  waiting for transfers between devices: 24.7 us -> 25.5 us
    dot_general x5 -> x3, matrix products: 6.19 us -> 1.59 us  [the longest x2 1.22 us: on_device(): out = jnp.dot(lhs, rhs, preferred_element_type=jnp.float32)]
    dot_general x4 -> x0, local copies, waits for them, and re-layouts: 4.28 us -> none  [the longest x2 4.21 us: on_device(): jnp.einsum('tij,tjf->tif', adjacency, blocks, preferred_element_type=jnp....]
    select_n x1 -> x3, other arithmetic: 0.08 us -> 3.39 us  [the longest x2 3.31 us: on_device(): jnp.where(placing[:, None, :, None], blocks[:, :, None, :], jnp.zeros((),...]
    ppermute x9 -> x6, starting transfers between devices: 9.92 us -> 6.72 us  [the longest x3 6.06 us: scatter_sum_pairs(): total = total + lax.ppermute(outgoing, axis, perm=perm)]
    ppermute x9 -> x6, waiting for transfers between devices: 9.78 us -> 12.9 us  [the longest x3 9.29 us: scatter_sum_pairs(): total = total + lax.ppermute(outgoing, axis, perm=perm)]
    unnamed x22 -> x31, local copies, waits for them, and re-layouts: 0.09 us -> 2.91 us
    ppermute x14, waiting for transfers between devices: 14.9 us -> 12.6 us  [gather_group(): received.append(lax.ppermute(block, axis, perm=perm))]
    reduce_sum x1 -> x0, other arithmetic: 1.41 us -> none  [on_device(): row_sums = jnp.sum(adjacency, axis=2, dtype=jnp.float32)]
  transfers between devices with their start and end apart: 23 -> 20, of which waited for: 11 -> 10; matrix products, arithmetic and copies ran while one was open for 1% -> 1% of each run, Pallas kernels for 0% -> 0%
where the time goes in v3:
time: 66.3 us; the launch traced here: 66.1 us
  starting transfers between devices  27.4 us (41%)
  waiting for transfers between devices  25.5 us (38%)
  local copies, waits for them, and re-layouts  6.02 us (9%)
  other arithmetic  4.21 us (6%)
  matrix products  1.97 us (3%)
  between operations  1.03 us (2%)
    ppermute x14, starting transfers between devices, gather_group(): received.append(lax.ppermute(block, axis, perm=perm))  20.7 us
    ppermute x14, waiting for transfers between devices, gather_group(): received.append(lax.ppermute(block, axis, perm=perm))  12.6 us
    ppermute x3, waiting for transfers between devices, scatter_sum_pairs(): total = total + lax.ppermute(outgoing, axis, perm=perm)  9.29 us
    ppermute x3, starting transfers between devices, scatter_sum_pairs(): total = total + lax.ppermute(outgoing, axis, perm=perm)  6.06 us
    ppermute x3, waiting for transfers between devices, scatter_sum_pairs(): half = mine + lax.ppermute(theirs, axis, perm=perm)  3.59 us
    select_n x2, other arithmetic, on_device(): jnp.where(placing[:, None, :, None], blocks[:, :, None, :], jnp.zeros((),...  3.31 us
    unnamed x31, local copies, waits for them, and re-layouts  2.91 us
  transfers between devices with their start and end apart: 20, of which 10 were waited for; matrix products, arithmetic and copies ran while one was open for 1% of the time, Pallas kernels for 0%

profile of v3, /device:TPU:0, one launch (start us, length us, event | category | flops | bytes accessed | tf_op | source)
XLA Modules:
  0.0 66.1 jit_solution(3964197903502185609)
XLA Ops:
  0.0 1.4 %copy.15 = bf16[1,1,6,256,256]{3,4,2,1,0:T(8,128)(2,1)S(1)} copy(bf16[1,1,6,256,256]{4,3,2,1,0:T(8,128)(2,1)} %param.10) | data formatting | bytes 1572864 | tf_op args[3]
  4.4 2.9 %collective-permute-start.1 = (f32[128]{0:T(128)S(1)}, f32[128]{0:T(128)S(1)}, u32[]{:S(2)}, u32[]{:S(2)}) collective-permute-start(f32[128]{0:T(128)S(1)} %fusion.27), channel_id=1, source_target_pairs={{0,16},{8,24},{16,0},{24,8},{1,17},{9,25},{17,1},{25,9},{2,18},{10... | collective-permute-start | bytes 1544 | tf_op jit(solution)/shard_map/ppermute | solution.py:61
  7.5 1.3 %collective-permute-done.1 = f32[128]{0:T(128)S(1)} collective-permute-done((f32[128]{0:T(128)S(1)}, f32[128]{0:T(128)S(1)}, u32[]{:S(2)}, u32[]{:S(2)}) %collective-permute-start.1) | collective-permute-done | bytes 544 | tf_op jit(solution)/shard_map/ppermute | solution.py:61
  9.0 5.1 %collective-permute-start.2 = (bf16[128,256]{1,0:T(8,128)(2,1)S(1)}, bf16[128,256]{1,0:T(8,128)(2,1)S(1)}, u32[]{:S(2)}, u32[]{:S(2)}) collective-permute-start(bf16[128,256]{1,0:T(8,128)(2,1)S(1)} %get-tuple-element.12), channel_id=1, source_target_pairs={{0,7},{1,0},{2,1},{3,2},{4,3},{5,4},{6,5},{7,6},{8,15},{9,8},{10,9... | collective-permute-start | bytes 196616 | tf_op jit(solution)/shard_map/ppermute | solution.py:14
  14.5 3.0 %collective-permute-start.5 = (bf16[128,256]{1,0:T(8,128)(2,1)S(1)}, bf16[128,256]{1,0:T(8,128)(2,1)S(1)}, u32[]{:S(2)}, u32[]{:S(2)}) collective-permute-start(bf16[128,256]{1,0:T(8,128)(2,1)S(1)} %get-tuple-element.12), channel_id=1, source_target_pairs={{0,4},{1,5},{2,6},{3,7},{4,0},{5,1},{6,2},{7,3},{8,12},{9,13},{10,... | collective-permute-start | bytes 196616 | tf_op jit(solution)/shard_map/ppermute | solution.py:14
  17.5 1.8 %collective-permute-start.7 = (bf16[128,256]{1,0:T(8,128)(2,1)S(1)}, bf16[128,256]{1,0:T(8,128)(2,1)S(1)}, u32[]{:S(2)}, u32[]{:S(2)}) collective-permute-start(bf16[128,256]{1,0:T(8,128)(2,1)S(1)} %get-tuple-element.12), channel_id=1, source_target_pairs={{0,2},{1,3},{2,4},{3,5},{4,6},{5,7},{6,0},{7,1},{8,10},{9,11},{10,... | collective-permute-start | bytes 196616 | tf_op jit(solution)/shard_map/ppermute | solution.py:14
  19.4 1.2 %collective-permute-start.8 = (bf16[128,256]{1,0:T(8,128)(2,1)S(1)}, bf16[128,256]{1,0:T(8,128)(2,1)S(1)}, u32[]{:S(2)}, u32[]{:S(2)}) collective-permute-start(bf16[128,256]{1,0:T(8,128)(2,1)S(1)} %get-tuple-element.12), channel_id=1, source_target_pairs={{0,1},{1,2},{2,3},{3,4},{4,5},{5,6},{6,7},{7,0},{8,9},{9,10},{10,1... | collective-permute-start | bytes 196616 | tf_op jit(solution)/shard_map/ppermute | solution.py:14
  20.6 2.9 %collective-permute-done.5 = bf16[128,256]{1,0:T(8,128)(2,1)S(1)} collective-permute-done((bf16[128,256]{1,0:T(8,128)(2,1)S(1)}, bf16[128,256]{1,0:T(8,128)(2,1)S(1)}, u32[]{:S(2)}, u32[]{:S(2)}) %collective-permute-start.5) | collective-permute-done | bytes 65568 | tf_op jit(solution)/shard_map/ppermute | solution.py:14
  23.5 3.9 %collective-permute-done.6 = bf16[128,256]{1,0:T(8,128)(2,1)S(1)} collective-permute-done((bf16[128,256]{1,0:T(8,128)(2,1)S(1)}, bf16[128,256]{1,0:T(8,128)(2,1)S(1)}, u32[]{:S(2)}, u32[]{:S(2)}) %collective-permute-start.6) | collective-permute-done | bytes 65568 | tf_op jit(solution)/shard_map/ppermute | solution.py:14
  28.0 1.7 %broadcast_select_fusion.1 = bf16[6,256,2,256]{3,2,1,0:T(2,128)(2,1)S(1)} fusion(pred[6,2]{1,0:T(8,128)(4,1)S(1)} %copy.14, bf16[6,256,256]{2,1,0:T(8,128)(2,1)S(1)} %bitcast.157), kind=kLoop, calls=%fused_computation.3 | loop fusion | flops 786432 | bytes 2359308 | tf_op jit(solution)/shard_map/jit(_where)/select_n | solution.py:103
  31.7 1.4 %collective-permute-done.9 = f32[2,128,256]{2,1,0:T(8,128)S(1)} collective-permute-done((f32[2,128,256]{2,1,0:T(8,128)S(1)}, f32[2,128,256]{2,1,0:T(8,128)S(1)}, u32[]{:S(2)}, u32[]{:S(2)}) %collective-permute-start.9) | collective-permute-done | bytes 262176 | tf_op jit(solution)/shard_map/ppermute | solution.py:55
  33.1 1.6 %collective-permute-start.10 = (f32[128,256]{1,0:T(8,128)S(1)}, f32[128,256]{1,0:T(8,128)S(1)}, u32[]{:S(2)}, u32[]{:S(2)}) collective-permute-start(f32[128,256]{1,0:T(8,128)S(1)} %dynamic-slice_bitcast_fusion.1), channel_id=1, source_target_pairs={{0,16},{8,24},{16,0},{24,8},{1,17},{9,25},{17,1},{25,9},{2,18},{10... | collective-permute-start | bytes 393224 | tf_op jit(solution)/shard_map/ppermute | solution.py:61
  34.7 4.0 %collective-permute-done.10 = f32[128,256]{1,0:T(8,128)S(1)} collective-permute-done((f32[128,256]{1,0:T(8,128)S(1)}, f32[128,256]{1,0:T(8,128)S(1)}, u32[]{:S(2)}, u32[]{:S(2)}) %collective-permute-start.10) | collective-permute-done | bytes 131104 | tf_op jit(solution)/shard_map/ppermute | solution.py:61
  39.0 2.0 %collective-permute-start.12 = (bf16[128,256]{1,0:T(8,128)(2,1)S(1)}, bf16[128,256]{1,0:T(8,128)(2,1)S(1)}, u32[]{:S(2)}, u32[]{:S(2)}) collective-permute-start(bf16[128,256]{1,0:T(8,128)(2,1)S(1)} %get-tuple-element.14), channel_id=1, source_target_pairs={{0,6},{1,7},{2,0},{3,1},{4,2},{5,3},{6,4},{7,5},{8,14},{9,15},{10,... | collective-permute-start | bytes 196616 | tf_op jit(solution)/shard_map/ppermute | solution.py:14
  41.7 2.1 %collective-permute-start.14 = (bf16[128,256]{1,0:T(8,128)(2,1)S(1)}, bf16[128,256]{1,0:T(8,128)(2,1)S(1)}, u32[]{:S(2)}, u32[]{:S(2)}) collective-permute-start(bf16[128,256]{1,0:T(8,128)(2,1)S(1)} %get-tuple-element.14), channel_id=1, source_target_pairs={{0,4},{1,5},{2,6},{3,7},{4,0},{5,1},{6,2},{7,3},{8,12},{9,13},{10,... | collective-permute-start | bytes 196616 | tf_op jit(solution)/shard_map/ppermute | solution.py:14
  43.8 0.9 %collective-permute-start.15 = (bf16[128,256]{1,0:T(8,128)(2,1)S(1)}, bf16[128,256]{1,0:T(8,128)(2,1)S(1)}, u32[]{:S(2)}, u32[]{:S(2)}) collective-permute-start(bf16[128,256]{1,0:T(8,128)(2,1)S(1)} %get-tuple-element.14), channel_id=1, source_target_pairs={{0,3},{1,4},{2,5},{3,6},{4,7},{5,0},{6,1},{7,2},{8,11},{9,12},{10,... | collective-permute-start | bytes 196616 | tf_op jit(solution)/shard_map/ppermute | solution.py:14
  44.8 1.4 %collective-permute-start.16 = (bf16[128,256]{1,0:T(8,128)(2,1)S(1)}, bf16[128,256]{1,0:T(8,128)(2,1)S(1)}, u32[]{:S(2)}, u32[]{:S(2)}) collective-permute-start(bf16[128,256]{1,0:T(8,128)(2,1)S(1)} %get-tuple-element.14), channel_id=1, source_target_pairs={{0,2},{1,3},{2,4},{3,5},{4,6},{5,7},{6,0},{7,1},{8,10},{9,11},{10,... | collective-permute-start | bytes 196616 | tf_op jit(solution)/shard_map/ppermute | solution.py:14
  46.1 2.0 %collective-permute-start.17 = (bf16[128,256]{1,0:T(8,128)(2,1)S(1)}, bf16[128,256]{1,0:T(8,128)(2,1)S(1)}, u32[]{:S(2)}, u32[]{:S(2)}) collective-permute-start(bf16[128,256]{1,0:T(8,128)(2,1)S(1)} %get-tuple-element.14), channel_id=1, source_target_pairs={{0,1},{1,2},{2,3},{3,4},{4,5},{5,6},{6,7},{7,0},{8,9},{9,10},{10,1... | collective-permute-start | bytes 196616 | tf_op jit(solution)/shard_map/ppermute | solution.py:14
  48.2 4.1 %collective-permute-done.14 = bf16[128,256]{1,0:T(8,128)(2,1)S(1)} collective-permute-done((bf16[128,256]{1,0:T(8,128)(2,1)S(1)}, bf16[128,256]{1,0:T(8,128)(2,1)S(1)}, u32[]{:S(2)}, u32[]{:S(2)}) %collective-permute-start.14) | collective-permute-done | bytes 65568 | tf_op jit(solution)/shard_map/ppermute | solution.py:14
  52.3 1.7 %collective-permute-done.15 = bf16[128,256]{1,0:T(8,128)(2,1)S(1)} collective-permute-done((bf16[128,256]{1,0:T(8,128)(2,1)S(1)}, bf16[128,256]{1,0:T(8,128)(2,1)S(1)}, u32[]{:S(2)}, u32[]{:S(2)}) %collective-permute-start.15) | collective-permute-done | bytes 65568 | tf_op jit(solution)/shard_map/ppermute | solution.py:14
  54.7 1.7 %broadcast_select_fusion = bf16[6,256,2,256]{3,2,1,0:T(2,128)(2,1)S(1)} fusion(pred[6,2]{1,0:T(8,128)(4,1)S(1)} %copy.14, bf16[6,256,256]{2,1,0:T(8,128)(2,1)S(1)} %bitcast.156), kind=kLoop, calls=%fused_computation.2 | loop fusion | flops 786432 | bytes 2359308 | tf_op jit(solution)/shard_map/jit(_where)/select_n | solution.py:103
  58.4 1.4 %collective-permute-done.18 = f32[2,128,256]{2,1,0:T(8,128)S(1)} collective-permute-done((f32[2,128,256]{2,1,0:T(8,128)S(1)}, f32[2,128,256]{2,1,0:T(8,128)S(1)}, u32[]{:S(2)}, u32[]{:S(2)}) %collective-permute-start.18) | collective-permute-done | bytes 262176 | tf_op jit(solution)/shard_map/ppermute | solution.py:55
  59.8 1.6 %collective-permute-start.19 = (f32[128,256]{1,0:T(8,128)S(1)}, f32[128,256]{1,0:T(8,128)S(1)}, u32[]{:S(2)}, u32[]{:S(2)}) collective-permute-start(f32[128,256]{1,0:T(8,128)S(1)} %dynamic-slice_bitcast_fusion), channel_id=1, source_target_pairs={{0,16},{8,24},{16,0},{24,8},{1,17},{9,25},{17,1},{25,9},{2,18},{10... | collective-permute-start | bytes 393224 | tf_op jit(solution)/shard_map/ppermute | solution.py:61
  61.4 4.0 %collective-permute-done.19 = f32[128,256]{1,0:T(8,128)S(1)} collective-permute-done((f32[128,256]{1,0:T(8,128)S(1)}, f32[128,256]{1,0:T(8,128)S(1)}, u32[]{:S(2)}, u32[]{:S(2)}) %collective-permute-start.19) | collective-permute-done | bytes 131104 | tf_op jit(solution)/shard_map/ppermute | solution.py:61
  (81 shorter events, 10.0 us)
Async XLA Ops:
  0.0 8.8 %copy-start = (bf16[128,256]{1,0:T(8,128)(2,1)S(1)}, bf16[128,256]{1,0:T(8,128)(2,1)}, u32[]{:S(2)}) copy-start(bf16[128,256]{1,0:T(8,128)(2,1)} %param.7) | copy-start | bytes 196612
  0.0 2.1 %copy-start.3 = (s32[1,1,6]{2,1,0:T(1,128)S(1)}, s32[1,1,6]{2,1,0:T(1,128)}, u32[]{:S(2)}) copy-start(s32[1,1,6]{2,1,0:T(1,128)} %param.11) | copy-start | bytes 76
  2.4 6.4 %copy-start.1 = (bf16[2,256,256]{2,1,0:T(8,128)(2,1)S(1)}, bf16[2,256,256]{2,1,0:T(8,128)(2,1)}, u32[]{:S(2)}) copy-start(bf16[2,256,256]{2,1,0:T(8,128)(2,1)} %param.8) | copy-start | bytes 786436
  3.0 1.3 %collective-permute-start = (f32[2,128]{1,0:T(2,128)S(1)}, f32[2,128]{1,0:T(2,128)S(1)}, u32[]{:S(2)}, u32[]{:S(2)}) collective-permute-start(f32[2,128]{1,0:T(2,128)S(1)} %fusion.23), channel_id=1, source_target_pairs={{0,8},{8,0},{16,24},{24,16},{1,9},{9,1},{17,25},{25,17},{2,10},{10... | collective-permute-start | bytes 3080 | tf_op jit(solution)/shard_map/ppermute | solution.py:55
  4.4 4.4 %collective-permute-start.1 = (f32[128]{0:T(128)S(1)}, f32[128]{0:T(128)S(1)}, u32[]{:S(2)}, u32[]{:S(2)}) collective-permute-start(f32[128]{0:T(128)S(1)} %fusion.27), channel_id=1, source_target_pairs={{0,16},{8,24},{16,0},{24,8},{1,17},{9,25},{17,1},{25,9},{2,18},{10... | collective-permute-start | bytes 1544 | tf_op jit(solution)/shard_map/ppermute | solution.py:61
  9.0 8.6 %collective-permute-start.2 = (bf16[128,256]{1,0:T(8,128)(2,1)S(1)}, bf16[128,256]{1,0:T(8,128)(2,1)S(1)}, u32[]{:S(2)}, u32[]{:S(2)}) collective-permute-start(bf16[128,256]{1,0:T(8,128)(2,1)S(1)} %get-tuple-element.12), channel_id=1, source_target_pairs={{0,7},{1,0},{2,1},{3,2},{4,3},{5,4},{6,5},{7,6},{8,15},{9,8},{10,9... | collective-permute-start | bytes 196616 | tf_op jit(solution)/shard_map/ppermute | solution.py:14
  14.1 5.3 %collective-permute-start.3 = (bf16[128,256]{1,0:T(8,128)(2,1)S(1)}, bf16[128,256]{1,0:T(8,128)(2,1)S(1)}, u32[]{:S(2)}, u32[]{:S(2)}) collective-permute-start(bf16[128,256]{1,0:T(8,128)(2,1)S(1)} %get-tuple-element.12), channel_id=1, source_target_pairs={{0,6},{1,7},{2,0},{3,1},{4,2},{5,3},{6,4},{7,5},{8,14},{9,15},{10,... | collective-permute-start | bytes 196616 | tf_op jit(solution)/shard_map/ppermute | solution.py:14
  14.5 6.1 %collective-permute-start.4 = (bf16[128,256]{1,0:T(8,128)(2,1)S(1)}, bf16[128,256]{1,0:T(8,128)(2,1)S(1)}, u32[]{:S(2)}, u32[]{:S(2)}) collective-permute-start(bf16[128,256]{1,0:T(8,128)(2,1)S(1)} %get-tuple-element.12), channel_id=1, source_target_pairs={{0,5},{1,6},{2,7},{3,0},{4,1},{5,2},{6,3},{7,4},{8,13},{9,14},{10,... | collective-permute-start | bytes 196616 | tf_op jit(solution)/shard_map/ppermute | solution.py:14
  14.5 8.9 %collective-permute-start.5 = (bf16[128,256]{1,0:T(8,128)(2,1)S(1)}, bf16[128,256]{1,0:T(8,128)(2,1)S(1)}, u32[]{:S(2)}, u32[]{:S(2)}) collective-permute-start(bf16[128,256]{1,0:T(8,128)(2,1)S(1)} %get-tuple-element.12), channel_id=1, source_target_pairs={{0,4},{1,5},{2,6},{3,7},{4,0},{5,1},{6,2},{7,3},{8,12},{9,13},{10,... | collective-permute-start | bytes 196616 | tf_op jit(solution)/shard_map/ppermute | solution.py:14
  17.5 9.8 %collective-permute-start.6 = (bf16[128,256]{1,0:T(8,128)(2,1)S(1)}, bf16[128,256]{1,0:T(8,128)(2,1)S(1)}, u32[]{:S(2)}, u32[]{:S(2)}) collective-permute-start(bf16[128,256]{1,0:T(8,128)(2,1)S(1)} %get-tuple-element.12), channel_id=1, source_target_pairs={{0,3},{1,4},{2,5},{3,6},{4,7},{5,0},{6,1},{7,2},{8,11},{9,12},{10,... | collective-permute-start | bytes 196616 | tf_op jit(solution)/shard_map/ppermute | solution.py:14
  17.5 9.8 %collective-permute-start.7 = (bf16[128,256]{1,0:T(8,128)(2,1)S(1)}, bf16[128,256]{1,0:T(8,128)(2,1)S(1)}, u32[]{:S(2)}, u32[]{:S(2)}) collective-permute-start(bf16[128,256]{1,0:T(8,128)(2,1)S(1)} %get-tuple-element.12), channel_id=1, source_target_pairs={{0,2},{1,3},{2,4},{3,5},{4,6},{5,7},{6,0},{7,1},{8,10},{9,11},{10,... | collective-permute-start | bytes 196616 | tf_op jit(solution)/shard_map/ppermute | solution.py:14
  19.4 8.0 %collective-permute-start.8 = (bf16[128,256]{1,0:T(8,128)(2,1)S(1)}, bf16[128,256]{1,0:T(8,128)(2,1)S(1)}, u32[]{:S(2)}, u32[]{:S(2)}) collective-permute-start(bf16[128,256]{1,0:T(8,128)(2,1)S(1)} %get-tuple-element.12), channel_id=1, source_target_pairs={{0,1},{1,2},{2,3},{3,4},{4,5},{5,6},{6,7},{7,0},{8,9},{9,10},{10,1... | collective-permute-start | bytes 196616 | tf_op jit(solution)/shard_map/ppermute | solution.py:14
  30.9 3.9 %copy-start.2 = (f32[2,256]{1,0:T(2,128)S(1)}, f32[2,256]{1,0:T(2,128)}, u32[]{:S(2)}) copy-start(f32[2,256]{1,0:T(2,128)} %param.9) | copy-start | bytes 6148
  31.5 1.6 %collective-permute-start.9 = (f32[2,128,256]{2,1,0:T(8,128)S(1)}, f32[2,128,256]{2,1,0:T(8,128)S(1)}, u32[]{:S(2)}, u32[]{:S(2)}) collective-permute-start(f32[2,128,256]{2,1,0:T(8,128)S(1)} %bitcast.165), channel_id=1, source_target_pairs={{0,8},{8,0},{16,24},{24,16},{1,9},{9,1},{17,25},{25,17},{2,10},{10... | collective-permute-start | bytes 786440 | tf_op jit(solution)/shard_map/ppermute | solution.py:55
  33.1 5.6 %collective-permute-start.10 = (f32[128,256]{1,0:T(8,128)S(1)}, f32[128,256]{1,0:T(8,128)S(1)}, u32[]{:S(2)}, u32[]{:S(2)}) collective-permute-start(f32[128,256]{1,0:T(8,128)S(1)} %dynamic-slice_bitcast_fusion.1), channel_id=1, source_target_pairs={{0,16},{8,24},{16,0},{24,8},{1,17},{9,25},{17,1},{25,9},{2,18},{10... | collective-permute-start | bytes 393224 | tf_op jit(solution)/shard_map/ppermute | solution.py:61
  39.0 5.8 %collective-permute-start.11 = (bf16[128,256]{1,0:T(8,128)(2,1)S(1)}, bf16[128,256]{1,0:T(8,128)(2,1)S(1)}, u32[]{:S(2)}, u32[]{:S(2)}) collective-permute-start(bf16[128,256]{1,0:T(8,128)(2,1)S(1)} %get-tuple-element.14), channel_id=1, source_target_pairs={{0,7},{1,0},{2,1},{3,2},{4,3},{5,4},{6,5},{7,6},{8,15},{9,8},{10,9... | collective-permute-start | bytes 196616 | tf_op jit(solution)/shard_map/ppermute | solution.py:14
  39.0 7.1 %collective-permute-start.12 = (bf16[128,256]{1,0:T(8,128)(2,1)S(1)}, bf16[128,256]{1,0:T(8,128)(2,1)S(1)}, u32[]{:S(2)}, u32[]{:S(2)}) collective-permute-start(bf16[128,256]{1,0:T(8,128)(2,1)S(1)} %get-tuple-element.14), channel_id=1, source_target_pairs={{0,6},{1,7},{2,0},{3,1},{4,2},{5,3},{6,4},{7,5},{8,14},{9,15},{10,... | collective-permute-start | bytes 196616 | tf_op jit(solution)/shard_map/ppermute | solution.py:14
  41.1 7.1 %collective-permute-start.13 = (bf16[128,256]{1,0:T(8,128)(2,1)S(1)}, bf16[128,256]{1,0:T(8,128)(2,1)S(1)}, u32[]{:S(2)}, u32[]{:S(2)}) collective-permute-start(bf16[128,256]{1,0:T(8,128)(2,1)S(1)} %get-tuple-element.14), channel_id=1, source_target_pairs={{0,5},{1,6},{2,7},{3,0},{4,1},{5,2},{6,3},{7,4},{8,13},{9,14},{10,... | collective-permute-start | bytes 196616 | tf_op jit(solution)/shard_map/ppermute | solution.py:14
  41.7 10.6 %collective-permute-start.14 = (bf16[128,256]{1,0:T(8,128)(2,1)S(1)}, bf16[128,256]{1,0:T(8,128)(2,1)S(1)}, u32[]{:S(2)}, u32[]{:S(2)}) collective-permute-start(bf16[128,256]{1,0:T(8,128)(2,1)S(1)} %get-tuple-element.14), channel_id=1, source_target_pairs={{0,4},{1,5},{2,6},{3,7},{4,0},{5,1},{6,2},{7,3},{8,12},{9,13},{10,... | collective-permute-start | bytes 196616 | tf_op jit(solution)/shard_map/ppermute | solution.py:14
  43.8 10.2 %collective-permute-start.15 = (bf16[128,256]{1,0:T(8,128)(2,1)S(1)}, bf16[128,256]{1,0:T(8,128)(2,1)S(1)}, u32[]{:S(2)}, u32[]{:S(2)}) collective-permute-start(bf16[128,256]{1,0:T(8,128)(2,1)S(1)} %get-tuple-element.14), channel_id=1, source_target_pairs={{0,3},{1,4},{2,5},{3,6},{4,7},{5,0},{6,1},{7,2},{8,11},{9,12},{10,... | collective-permute-start | bytes 196616 | tf_op jit(solution)/shard_map/ppermute | solution.py:14
  44.8 9.3 %collective-permute-start.16 = (bf16[128,256]{1,0:T(8,128)(2,1)S(1)}, bf16[128,256]{1,0:T(8,128)(2,1)S(1)}, u32[]{:S(2)}, u32[]{:S(2)}) collective-permute-start(bf16[128,256]{1,0:T(8,128)(2,1)S(1)} %get-tuple-element.14), channel_id=1, source_target_pairs={{0,2},{1,3},{2,4},{3,5},{4,6},{5,7},{6,0},{7,1},{8,10},{9,11},{10,... | collective-permute-start | bytes 196616 | tf_op jit(solution)/shard_map/ppermute | solution.py:14
  46.1 7.9 %collective-permute-start.17 = (bf16[128,256]{1,0:T(8,128)(2,1)S(1)}, bf16[128,256]{1,0:T(8,128)(2,1)S(1)}, u32[]{:S(2)}, u32[]{:S(2)}) collective-permute-start(bf16[128,256]{1,0:T(8,128)(2,1)S(1)} %get-tuple-element.14), channel_id=1, source_target_pairs={{0,1},{1,2},{2,3},{3,4},{4,5},{5,6},{6,7},{7,0},{8,9},{9,10},{10,1... | collective-permute-start | bytes 196616 | tf_op jit(solution)/shard_map/ppermute | solution.py:14
  58.2 1.6 %collective-permute-start.18 = (f32[2,128,256]{2,1,0:T(8,128)S(1)}, f32[2,128,256]{2,1,0:T(8,128)S(1)}, u32[]{:S(2)}, u32[]{:S(2)}) collective-permute-start(f32[2,128,256]{2,1,0:T(8,128)S(1)} %bitcast.166), channel_id=1, source_target_pairs={{0,8},{8,0},{16,24},{24,16},{1,9},{9,1},{17,25},{25,17},{2,10},{10... | collective-permute-start | bytes 786440 | tf_op jit(solution)/shard_map/ppermute | solution.py:55
  59.8 5.6 %collective-permute-start.19 = (f32[128,256]{1,0:T(8,128)S(1)}, f32[128,256]{1,0:T(8,128)S(1)}, u32[]{:S(2)}, u32[]{:S(2)}) collective-permute-start(f32[128,256]{1,0:T(8,128)S(1)} %dynamic-slice_bitcast_fusion), channel_id=1, source_target_pairs={{0,16},{8,24},{16,0},{24,8},{1,17},{9,25},{17,1},{25,9},{2,18},{10... | collective-permute-start | bytes 393224 | tf_op jit(solution)/shard_map/ppermute | solution.py:61
  (1 other events, 1.2 us)

commit v4 on v3

--- a/solution.py
+++ b/solution.py
@@ -4,7 +4,8 @@
 from jax.sharding import PartitionSpec as P
 
 LAYERS = 2
-TWO_STAGE_GATHER = False
+TWO_STAGE_GATHER = True
+SPLIT = True
 
 
 def gather_group(block, axis, size):
@@ -31,6 +32,26 @@
         perm = [(i, (i - shift * per_tile) % size) for i in range(size)]
         tiles.append(lax.ppermute(tile, axis, perm=perm))
     return jnp.stack(tiles)
+
+
+def gather_outer_first(block, axis, size, per_tile, split):
+    me = lax.axis_index(axis)
+    pos = me % per_tile
+    n_tiles = size // per_tile
+    outer = [block]
+    for shift in range(1, n_tiles):
+        perm = [(i, (i - shift * per_tile) % size) for i in range(size)]
+        outer.append(lax.ppermute(block, axis, perm=perm))
+    full = [jnp.stack(outer)]
+    for shift in range(1, per_tile):
+        perm = [(i, i - i % per_tile + (i - shift) % per_tile) for i in range(size)]
+        if split:
+            full.append(jnp.stack([lax.ppermute(part, axis, perm=perm) for part in outer]))
+        else:
+            full.append(lax.ppermute(full[0], axis, perm=perm))
+    stacked = jnp.stack(full)
+    order = (lax.iota(jnp.int32, per_tile) - pos) % per_tile
+    return jnp.swapaxes(stacked[order], 0, 1)
 
 
 def scatter_sum(parts, axis, size):
@@ -78,6 +99,10 @@
     live = lax.iota(jnp.int32, slots) < count_here
     placing = (rows_here[:, None] == lax.iota(jnp.int32, row_tiles)[None, :]) & live[:, None]
     lhs = adjacency.transpose(1, 0, 2).reshape(tile_size, slots * tile_size)
+    slot_mask = jnp.broadcast_to(placing.T[:, None, :, None], (row_tiles, 1, slots, tile_size))
+    placed_lhs = jnp.where(
+        slot_mask.reshape(row_tiles, 1, slots * tile_size), lhs[None], jnp.zeros((), lhs.dtype)
+    ).reshape(row_tiles * tile_size, slots * tile_size)
     pick = jnp.broadcast_to(placing[:, None, :, None], (slots, tile_size, row_tiles, 128))
     row_sums = jnp.dot(
         lhs, pick.astype(adjacency.dtype).reshape(slots * tile_size, row_tiles * 128),
@@ -93,21 +118,17 @@
         mixed = jnp.dot(hidden, weights[layer_index], preferred_element_type=jnp.float32)
         scaled = (mixed * scale).astype(jnp.bfloat16)
         if TWO_STAGE_GATHER and per_tile > 1 and grp_size % per_tile == 0:
-            tiles = gather_tiles(scaled, "grp", grp_size, per_tile)
+            tiles = gather_outer_first(scaled, "grp", grp_size, per_tile, SPLIT)
             n_tiles = grp_size // per_tile
             blocks = tiles[(cols_here - me_grp // per_tile) % n_tiles].reshape(slots, tile_size, width)
         else:
             received = gather_group(scaled, "grp", grp_size)
             sources = cols_here[:, None] * per_tile + lax.iota(jnp.int32, per_tile)[None, :]
             blocks = received[(sources - me_grp) % grp_size].reshape(slots, tile_size, width)
-        rhs = jnp.where(
-            placing[:, None, :, None], blocks[:, :, None, :], jnp.zeros((), blocks.dtype)
-        ).reshape(slots * tile_size, row_tiles * width)
-        out = jnp.dot(lhs, rhs, preferred_element_type=jnp.float32)
-        partial_value = (
-            out.reshape(per_tile, node_dev, row_tiles, width).transpose(2, 0, 1, 3)
-            .reshape(blk_size, node_dev, width)
+        out = jnp.dot(
+            placed_lhs, blocks.reshape(slots * tile_size, width), preferred_element_type=jnp.float32
         )
+        partial_value = out.reshape(blk_size, node_dev, width)
         summed = scatter_sum_pairs(partial_value, "blk", blk_size)
         pre = (summed + scaled.astype(jnp.float32)) * scale + biases[layer_index][None, :]
         if layer_index < LAYERS - 1:

time: 66.3 us -> 55.7 us (0.84)
  waiting for transfers between devices: 25.5 us -> 21.8 us
  starting transfers between devices: 27.4 us -> 24.9 us
  other arithmetic: 4.21 us -> 1.75 us
  local copies, waits for them, and re-layouts: 6.02 us -> 4.06 us
    select_n x3 -> x2, other arithmetic: 3.39 us -> 0.03 us  [the longest x1 0.01 us: on_device(): tiles[(cols_here - me_grp // per_tile) % n_tiles]]
    ppermute x14, waiting for transfers between devices: 12.6 us -> 9.43 us  [the longest x8 6.61 us: gather_outer_first(): lax.ppermute(part, axis, perm=perm)]
    ppermute x14, starting transfers between devices: 20.7 us -> 18.2 us  [the longest x6 9.94 us: gather_outer_first(): outer.append(lax.ppermute(block, axis, perm=perm))]
    unnamed x31 -> x17, local copies, waits for them, and re-layouts: 2.91 us -> 0.59 us
    gather x2 -> x4, local copies, waits for them, and re-layouts: 1.19 us -> 2.36 us  [the longest x2 1.19 us: on_device(): tiles[(cols_here - me_grp // per_tile) % n_tiles]]
    another operation x4 -> x0, local copies, waits for them, and re-layouts: 0.93 us -> none
    broadcast_in_dim x0 -> x2, local copies, waits for them, and re-layouts: none -> 0.79 us  [on_device(): jnp.where(slot_mask.reshape(row_tiles, 1, slots * tile_size), lhs[None],...]
    and x1 -> x2, other arithmetic: 0.01 us -> 0.67 us  [on_device(): (rows_here[:, None] == lax.iota(jnp.int32, row_tiles)[None, :]) & live[:,...]
  transfers between devices with their start and end apart: 20 -> 20, of which waited for: 10 -> 15; matrix products, arithmetic and copies ran while one was open for 1% -> 2% of each run, Pallas kernels for 0% -> 0%
where the time goes in v4:
time: 55.7 us; the launch traced here: 55.5 us
  starting transfers between devices  24.9 us (45%)
  waiting for transfers between devices  21.8 us (39%)
  local copies, waits for them, and re-layouts  4.06 us (7%)
  matrix products  1.87 us (3%)
  other arithmetic  1.75 us (3%)
  between operations  1.12 us (2%)
    ppermute x6, starting transfers between devices, gather_outer_first(): outer.append(lax.ppermute(block, axis, perm=perm))  9.94 us
    ppermute x3, waiting for transfers between devices, scatter_sum_pairs(): total = total + lax.ppermute(outgoing, axis, perm=perm)  8.7 us
    ppermute x8, starting transfers between devices, gather_outer_first(): lax.ppermute(part, axis, perm=perm)  8.24 us
    ppermute x8, waiting for transfers between devices, gather_outer_first(): lax.ppermute(part, axis, perm=perm)  6.61 us
    ppermute x3, starting transfers between devices, scatter_sum_pairs(): total = total + lax.ppermute(outgoing, axis, perm=perm)  6.06 us
    ppermute x3, waiting for transfers between devices, scatter_sum_pairs(): half = mine + lax.ppermute(theirs, axis, perm=perm)  3.71 us
    ppermute x6, waiting for transfers between devices, gather_outer_first(): outer.append(lax.ppermute(block, axis, perm=perm))  2.81 us
    gather x2, local copies, waits for them, and re-layouts, on_device(): tiles[(cols_here - me_grp // per_tile) % n_tiles]  1.19 us
  transfers between devices with their start and end apart: 20, of which 15 were waited for; matrix products, arithmetic and copies ran while one was open for 2% of the time, Pallas kernels for 0%

profile of v4, /device:TPU:0, one launch (start us, length us, event | category | flops | bytes accessed | tf_op | source)
XLA Modules:
  0.0 55.5 jit_solution(18273503294462911248)
XLA Ops:
  3.9 2.9 %collective-permute-start.1 = (f32[128]{0:T(128)S(1)}, f32[128]{0:T(128)S(1)}, u32[]{:S(2)}, u32[]{:S(2)}) collective-permute-start(f32[128]{0:T(128)S(1)} %fusion.40), channel_id=1, source_target_pairs={{0,16},{8,24},{16,0},{24,8},{1,17},{9,25},{17,1},{25,9},{2,18},{10... | collective-permute-start | bytes 1544 | tf_op jit(solution)/shard_map/ppermute | solution.py:82
  8.5 2.1 %collective-permute-start.4 = (bf16[128,256]{1,0:T(8,128)(2,1)S(1)}, bf16[128,256]{1,0:T(8,128)(2,1)S(1)}, u32[]{:S(2)}, u32[]{:S(2)}) collective-permute-start(bf16[128,256]{1,0:T(8,128)(2,1)S(1)} %fusion.6), channel_id=1, source_target_pairs={{0,2},{1,3},{2,4},{3,5},{4,6},{5,7},{6,0},{7,1},{8,10},{9,11},{10,... | collective-permute-start | bytes 196616 | tf_op jit(solution)/shard_map/ppermute | solution.py:44
  10.7 2.6 %collective-permute-start.3 = (bf16[128,256]{1,0:T(8,128)(2,1)S(1)}, bf16[128,256]{1,0:T(8,128)(2,1)S(1)}, u32[]{:S(2)}, u32[]{:S(2)}) collective-permute-start(bf16[128,256]{1,0:T(8,128)(2,1)S(1)} %fusion.6), channel_id=1, source_target_pairs={{0,4},{1,5},{2,6},{3,7},{4,0},{5,1},{6,2},{7,3},{8,12},{9,13},{10,... | collective-permute-start | bytes 196616 | tf_op jit(solution)/shard_map/ppermute | solution.py:44
  13.2 1.3 %collective-permute-start.2 = (bf16[128,256]{1,0:T(8,128)(2,1)S(1)}, bf16[128,256]{1,0:T(8,128)(2,1)S(1)}, u32[]{:S(2)}, u32[]{:S(2)}) collective-permute-start(bf16[128,256]{1,0:T(8,128)(2,1)S(1)} %fusion.6), channel_id=1, source_target_pairs={{0,6},{1,7},{2,0},{3,1},{4,2},{5,3},{6,4},{7,5},{8,14},{9,15},{10,... | collective-permute-start | bytes 196616 | tf_op jit(solution)/shard_map/ppermute | solution.py:44
  14.6 1.5 %collective-permute-start.5 = (bf16[128,256]{1,0:T(8,128)(2,1)S(1)}, bf16[128,256]{1,0:T(8,128)(2,1)S(1)}, u32[]{:S(2)}, u32[]{:S(2)}) collective-permute-start(bf16[128,256]{1,0:T(8,128)(2,1)S(1)} %fusion.6), channel_id=1, source_target_pairs={{0,1},{1,0},{2,3},{3,2},{4,5},{5,4},{6,7},{7,6},{8,9},{9,8},{10,11... | collective-permute-start | bytes 196616 | tf_op jit(solution)/shard_map/ppermute | solution.py:49
  16.1 1.2 %collective-permute-start.8 = (bf16[128,256]{1,0:T(8,128)(2,1)S(1)}, bf16[128,256]{1,0:T(8,128)(2,1)S(1)}, u32[]{:S(2)}, u32[]{:S(2)}) collective-permute-start(bf16[128,256]{1,0:T(8,128)(2,1)S(1)} %collective-permute-done.4), channel_id=1, source_target_pairs={{0,1},{1,0},{2,3},{3,2},{4,5},{5,4},{6,7},{7,6},{8,9},{9,8},{10,11... | collective-permute-start | bytes 196616 | tf_op jit(solution)/shard_map/ppermute | solution.py:49
  17.6 1.5 %collective-permute-start.7 = (bf16[128,256]{1,0:T(8,128)(2,1)S(1)}, bf16[128,256]{1,0:T(8,128)(2,1)S(1)}, u32[]{:S(2)}, u32[]{:S(2)}) collective-permute-start(bf16[128,256]{1,0:T(8,128)(2,1)S(1)} %collective-permute-done.3), channel_id=1, source_target_pairs={{0,1},{1,0},{2,3},{3,2},{4,5},{5,4},{6,7},{7,6},{8,9},{9,8},{10,11... | collective-permute-start | bytes 196616 | tf_op jit(solution)/shard_map/ppermute | solution.py:49
  20.4 1.5 %collective-permute-done.7 = bf16[128,256]{1,0:T(8,128)(2,1)S(1)} collective-permute-done((bf16[128,256]{1,0:T(8,128)(2,1)S(1)}, bf16[128,256]{1,0:T(8,128)(2,1)S(1)}, u32[]{:S(2)}, u32[]{:S(2)}) %collective-permute-start.7) | collective-permute-done | bytes 65568 | tf_op jit(solution)/shard_map/ppermute | solution.py:49
  21.9 1.5 %collective-permute-done.6 = bf16[128,256]{1,0:T(8,128)(2,1)S(1)} collective-permute-done((bf16[128,256]{1,0:T(8,128)(2,1)S(1)}, bf16[128,256]{1,0:T(8,128)(2,1)S(1)}, u32[]{:S(2)}, u32[]{:S(2)}) %collective-permute-start.6) | collective-permute-done | bytes 65568 | tf_op jit(solution)/shard_map/ppermute | solution.py:49
  25.4 1.5 %collective-permute-done.9 = f32[2,128,256]{2,1,0:T(8,128)S(1)} collective-permute-done((f32[2,128,256]{2,1,0:T(8,128)S(1)}, f32[2,128,256]{2,1,0:T(8,128)S(1)}, u32[]{:S(2)}, u32[]{:S(2)}) %collective-permute-start.9) | collective-permute-done | bytes 262176 | tf_op jit(solution)/shard_map/ppermute | solution.py:76
  26.9 1.6 %collective-permute-start.10 = (f32[128,256]{1,0:T(8,128)S(1)}, f32[128,256]{1,0:T(8,128)S(1)}, u32[]{:S(2)}, u32[]{:S(2)}) collective-permute-start(f32[128,256]{1,0:T(8,128)S(1)} %dynamic-slice_bitcast_fusion.3), channel_id=1, source_target_pairs={{0,16},{8,24},{16,0},{24,8},{1,17},{9,25},{17,1},{25,9},{2,18},{10... | collective-permute-start | bytes 393224 | tf_op jit(solution)/shard_map/ppermute | solution.py:82
  28.5 4.0 %collective-permute-done.10 = f32[128,256]{1,0:T(8,128)S(1)} collective-permute-done((f32[128,256]{1,0:T(8,128)S(1)}, f32[128,256]{1,0:T(8,128)S(1)}, u32[]{:S(2)}, u32[]{:S(2)}) %collective-permute-start.10) | collective-permute-done | bytes 131104 | tf_op jit(solution)/shard_map/ppermute | solution.py:82
  32.8 2.6 %collective-permute-start.12 = (bf16[128,256]{1,0:T(8,128)(2,1)S(1)}, bf16[128,256]{1,0:T(8,128)(2,1)S(1)}, u32[]{:S(2)}, u32[]{:S(2)}) collective-permute-start(bf16[128,256]{1,0:T(8,128)(2,1)S(1)} %fusion.7), channel_id=1, source_target_pairs={{0,4},{1,5},{2,6},{3,7},{4,0},{5,1},{6,2},{7,3},{8,12},{9,13},{10,... | collective-permute-start | bytes 196616 | tf_op jit(solution)/shard_map/ppermute | solution.py:44
  35.4 1.2 %collective-permute-start.11 = (bf16[128,256]{1,0:T(8,128)(2,1)S(1)}, bf16[128,256]{1,0:T(8,128)(2,1)S(1)}, u32[]{:S(2)}, u32[]{:S(2)}) collective-permute-start(bf16[128,256]{1,0:T(8,128)(2,1)S(1)} %fusion.7), channel_id=1, source_target_pairs={{0,6},{1,7},{2,0},{3,1},{4,2},{5,3},{6,4},{7,5},{8,14},{9,15},{10,... | collective-permute-start | bytes 196616 | tf_op jit(solution)/shard_map/ppermute | solution.py:44
  36.6 0.9 %collective-permute-start.14 = (bf16[128,256]{1,0:T(8,128)(2,1)S(1)}, bf16[128,256]{1,0:T(8,128)(2,1)S(1)}, u32[]{:S(2)}, u32[]{:S(2)}) collective-permute-start(bf16[128,256]{1,0:T(8,128)(2,1)S(1)} %fusion.7), channel_id=1, source_target_pairs={{0,1},{1,0},{2,3},{3,2},{4,5},{5,4},{6,7},{7,6},{8,9},{9,8},{10,11... | collective-permute-start | bytes 196616 | tf_op jit(solution)/shard_map/ppermute | solution.py:49
  37.5 1.8 %collective-permute-done.13 = bf16[128,256]{1,0:T(8,128)(2,1)S(1)} collective-permute-done((bf16[128,256]{1,0:T(8,128)(2,1)S(1)}, bf16[128,256]{1,0:T(8,128)(2,1)S(1)}, u32[]{:S(2)}, u32[]{:S(2)}) %collective-permute-start.13) | collective-permute-done | bytes 65568 | tf_op jit(solution)/shard_map/ppermute | solution.py:44
  40.7 0.7 %collective-permute-start.16 = (bf16[128,256]{1,0:T(8,128)(2,1)S(1)}, bf16[128,256]{1,0:T(8,128)(2,1)S(1)}, u32[]{:S(2)}, u32[]{:S(2)}) collective-permute-start(bf16[128,256]{1,0:T(8,128)(2,1)S(1)} %collective-permute-done.12), channel_id=1, source_target_pairs={{0,1},{1,0},{2,3},{3,2},{4,5},{5,4},{6,7},{7,6},{8,9},{9,8},{10,11... | collective-permute-start | bytes 196616 | tf_op jit(solution)/shard_map/ppermute | solution.py:49
  41.4 1.3 %collective-permute-start.15 = (bf16[128,256]{1,0:T(8,128)(2,1)S(1)}, bf16[128,256]{1,0:T(8,128)(2,1)S(1)}, u32[]{:S(2)}, u32[]{:S(2)}) collective-permute-start(bf16[128,256]{1,0:T(8,128)(2,1)S(1)} %collective-permute-done.11), channel_id=1, source_target_pairs={{0,1},{1,0},{2,3},{3,2},{4,5},{5,4},{6,7},{7,6},{8,9},{9,8},{10,11... | collective-permute-start | bytes 196616 | tf_op jit(solution)/shard_map/ppermute | solution.py:49
  42.7 0.9 %collective-permute-done.17 = bf16[128,256]{1,0:T(8,128)(2,1)S(1)} collective-permute-done((bf16[128,256]{1,0:T(8,128)(2,1)S(1)}, bf16[128,256]{1,0:T(8,128)(2,1)S(1)}, u32[]{:S(2)}, u32[]{:S(2)}) %collective-permute-start.17) | collective-permute-done | bytes 65568 | tf_op jit(solution)/shard_map/ppermute | solution.py:49
  43.6 1.3 %collective-permute-done.16 = bf16[128,256]{1,0:T(8,128)(2,1)S(1)} collective-permute-done((bf16[128,256]{1,0:T(8,128)(2,1)S(1)}, bf16[128,256]{1,0:T(8,128)(2,1)S(1)}, u32[]{:S(2)}, u32[]{:S(2)}) %collective-permute-start.16) | collective-permute-done | bytes 65568 | tf_op jit(solution)/shard_map/ppermute | solution.py:49
  44.9 0.7 %collective-permute-done.15 = bf16[128,256]{1,0:T(8,128)(2,1)S(1)} collective-permute-done((bf16[128,256]{1,0:T(8,128)(2,1)S(1)}, bf16[128,256]{1,0:T(8,128)(2,1)S(1)}, u32[]{:S(2)}, u32[]{:S(2)}) %collective-permute-start.15) | collective-permute-done | bytes 65568 | tf_op jit(solution)/shard_map/ppermute | solution.py:49
  47.6 1.5 %collective-permute-done.18 = f32[2,128,256]{2,1,0:T(8,128)S(1)} collective-permute-done((f32[2,128,256]{2,1,0:T(8,128)S(1)}, f32[2,128,256]{2,1,0:T(8,128)S(1)}, u32[]{:S(2)}, u32[]{:S(2)}) %collective-permute-start.18) | collective-permute-done | bytes 262176 | tf_op jit(solution)/shard_map/ppermute | solution.py:76
  49.2 1.6 %collective-permute-start.19 = (f32[128,256]{1,0:T(8,128)S(1)}, f32[128,256]{1,0:T(8,128)S(1)}, u32[]{:S(2)}, u32[]{:S(2)}) collective-permute-start(f32[128,256]{1,0:T(8,128)S(1)} %dynamic-slice_bitcast_fusion.2), channel_id=1, source_target_pairs={{0,16},{8,24},{16,0},{24,8},{1,17},{9,25},{17,1},{25,9},{2,18},{10... | collective-permute-start | bytes 393224 | tf_op jit(solution)/shard_map/ppermute | solution.py:82
  50.8 4.0 %collective-permute-done.19 = f32[128,256]{1,0:T(8,128)S(1)} collective-permute-done((f32[128,256]{1,0:T(8,128)S(1)}, f32[128,256]{1,0:T(8,128)S(1)}, u32[]{:S(2)}, u32[]{:S(2)}) %collective-permute-start.19) | collective-permute-done | bytes 131104 | tf_op jit(solution)/shard_map/ppermute | solution.py:82
  (71 shorter events, 12.6 us)
Async XLA Ops:
  0.0 8.3 %copy-start = (bf16[128,256]{1,0:T(8,128)(2,1)S(1)}, bf16[128,256]{1,0:T(8,128)(2,1)}, u32[]{:S(2)}) copy-start(bf16[128,256]{1,0:T(8,128)(2,1)} %param.7) | copy-start | bytes 196612
  0.0 1.8 %copy-start.1 = (bf16[1,1,6,256,256]{4,3,2,1,0:T(8,128)(2,1)S(1)}, bf16[1,1,6,256,256]{4,3,2,1,0:T(8,128)(2,1)}, u32[]{:S(2)}) copy-start(bf16[1,1,6,256,256]{4,3,2,1,0:T(8,128)(2,1)} %param.10) | copy-start | bytes 2359300
  2.6 1.3 %collective-permute-start = (f32[2,128]{1,0:T(2,128)S(1)}, f32[2,128]{1,0:T(2,128)S(1)}, u32[]{:S(2)}, u32[]{:S(2)}) collective-permute-start(f32[2,128]{1,0:T(2,128)S(1)} %fusion.32), channel_id=1, source_target_pairs={{0,8},{8,0},{16,24},{24,16},{1,9},{9,1},{17,25},{25,17},{2,10},{10... | collective-permute-start | bytes 3080 | tf_op jit(solution)/shard_map/ppermute | solution.py:76
  3.9 4.4 %collective-permute-start.1 = (f32[128]{0:T(128)S(1)}, f32[128]{0:T(128)S(1)}, u32[]{:S(2)}, u32[]{:S(2)}) collective-permute-start(f32[128]{0:T(128)S(1)} %fusion.40), channel_id=1, source_target_pairs={{0,16},{8,24},{16,0},{24,8},{1,17},{9,25},{17,1},{25,9},{2,18},{10... | collective-permute-start | bytes 1544 | tf_op jit(solution)/shard_map/ppermute | solution.py:82
  7.0 1.3 %copy-start.2 = (bf16[2,256,256]{2,1,0:T(8,128)(2,1)S(1)}, bf16[2,256,256]{2,1,0:T(8,128)(2,1)}, u32[]{:S(2)}) copy-start(bf16[2,256,256]{2,1,0:T(8,128)(2,1)} %param.8) | copy-start | bytes 786436
  8.5 7.6 %collective-permute-start.4 = (bf16[128,256]{1,0:T(8,128)(2,1)S(1)}, bf16[128,256]{1,0:T(8,128)(2,1)S(1)}, u32[]{:S(2)}, u32[]{:S(2)}) collective-permute-start(bf16[128,256]{1,0:T(8,128)(2,1)S(1)} %fusion.6), channel_id=1, source_target_pairs={{0,2},{1,3},{2,4},{3,5},{4,6},{5,7},{6,0},{7,1},{8,10},{9,11},{10,... | collective-permute-start | bytes 196616 | tf_op jit(solution)/shard_map/ppermute | solution.py:44
  10.7 6.9 %collective-permute-start.3 = (bf16[128,256]{1,0:T(8,128)(2,1)S(1)}, bf16[128,256]{1,0:T(8,128)(2,1)S(1)}, u32[]{:S(2)}, u32[]{:S(2)}) collective-permute-start(bf16[128,256]{1,0:T(8,128)(2,1)S(1)} %fusion.6), channel_id=1, source_target_pairs={{0,4},{1,5},{2,6},{3,7},{4,0},{5,1},{6,2},{7,3},{8,12},{9,13},{10,... | collective-permute-start | bytes 196616 | tf_op jit(solution)/shard_map/ppermute | solution.py:44
  13.2 5.8 %collective-permute-start.2 = (bf16[128,256]{1,0:T(8,128)(2,1)S(1)}, bf16[128,256]{1,0:T(8,128)(2,1)S(1)}, u32[]{:S(2)}, u32[]{:S(2)}) collective-permute-start(bf16[128,256]{1,0:T(8,128)(2,1)S(1)} %fusion.6), channel_id=1, source_target_pairs={{0,6},{1,7},{2,0},{3,1},{4,2},{5,3},{6,4},{7,5},{8,14},{9,15},{10,... | collective-permute-start | bytes 196616 | tf_op jit(solution)/shard_map/ppermute | solution.py:44
  14.6 5.1 %collective-permute-start.5 = (bf16[128,256]{1,0:T(8,128)(2,1)S(1)}, bf16[128,256]{1,0:T(8,128)(2,1)S(1)}, u32[]{:S(2)}, u32[]{:S(2)}) collective-permute-start(bf16[128,256]{1,0:T(8,128)(2,1)S(1)} %fusion.6), channel_id=1, source_target_pairs={{0,1},{1,0},{2,3},{3,2},{4,5},{5,4},{6,7},{7,6},{8,9},{9,8},{10,11... | collective-permute-start | bytes 196616 | tf_op jit(solution)/shard_map/ppermute | solution.py:49
  16.1 4.3 %collective-permute-start.8 = (bf16[128,256]{1,0:T(8,128)(2,1)S(1)}, bf16[128,256]{1,0:T(8,128)(2,1)S(1)}, u32[]{:S(2)}, u32[]{:S(2)}) collective-permute-start(bf16[128,256]{1,0:T(8,128)(2,1)S(1)} %collective-permute-done.4), channel_id=1, source_target_pairs={{0,1},{1,0},{2,3},{3,2},{4,5},{5,4},{6,7},{7,6},{8,9},{9,8},{10,11... | collective-permute-start | bytes 196616 | tf_op jit(solution)/shard_map/ppermute | solution.py:49
  17.6 4.3 %collective-permute-start.7 = (bf16[128,256]{1,0:T(8,128)(2,1)S(1)}, bf16[128,256]{1,0:T(8,128)(2,1)S(1)}, u32[]{:S(2)}, u32[]{:S(2)}) collective-permute-start(bf16[128,256]{1,0:T(8,128)(2,1)S(1)} %collective-permute-done.3), channel_id=1, source_target_pairs={{0,1},{1,0},{2,3},{3,2},{4,5},{5,4},{6,7},{7,6},{8,9},{9,8},{10,11... | collective-permute-start | bytes 196616 | tf_op jit(solution)/shard_map/ppermute | solution.py:49
  19.1 4.3 %collective-permute-start.6 = (bf16[128,256]{1,0:T(8,128)(2,1)S(1)}, bf16[128,256]{1,0:T(8,128)(2,1)S(1)}, u32[]{:S(2)}, u32[]{:S(2)}) collective-permute-start(bf16[128,256]{1,0:T(8,128)(2,1)S(1)} %collective-permute-done.2), channel_id=1, source_target_pairs={{0,1},{1,0},{2,3},{3,2},{4,5},{5,4},{6,7},{7,6},{8,9},{9,8},{10,11... | collective-permute-start | bytes 196616 | tf_op jit(solution)/shard_map/ppermute | solution.py:49
  25.2 3.3 %copy-start.3 = (f32[2,256]{1,0:T(2,128)S(1)}, f32[2,256]{1,0:T(2,128)}, u32[]{:S(2)}) copy-start(f32[2,256]{1,0:T(2,128)} %param.9) | copy-start | bytes 6148
  25.3 1.6 %collective-permute-start.9 = (f32[2,128,256]{2,1,0:T(8,128)S(1)}, f32[2,128,256]{2,1,0:T(8,128)S(1)}, u32[]{:S(2)}, u32[]{:S(2)}) collective-permute-start(f32[2,128,256]{2,1,0:T(8,128)S(1)} %dynamic-slice_bitcast_fusion.1), channel_id=1, source_target_pairs={{0,8},{8,0},{16,24},{24,16},{1,9},{9,1},{17,25},{25,17},{2,10},{10... | collective-permute-start | bytes 786440 | tf_op jit(solution)/shard_map/ppermute | solution.py:76
  26.9 5.6 %collective-permute-start.10 = (f32[128,256]{1,0:T(8,128)S(1)}, f32[128,256]{1,0:T(8,128)S(1)}, u32[]{:S(2)}, u32[]{:S(2)}) collective-permute-start(f32[128,256]{1,0:T(8,128)S(1)} %dynamic-slice_bitcast_fusion.3), channel_id=1, source_target_pairs={{0,16},{8,24},{16,0},{24,8},{1,17},{9,25},{17,1},{25,9},{2,18},{10... | collective-permute-start | bytes 393224 | tf_op jit(solution)/shard_map/ppermute | solution.py:82
  32.8 6.6 %collective-permute-start.13 = (bf16[128,256]{1,0:T(8,128)(2,1)S(1)}, bf16[128,256]{1,0:T(8,128)(2,1)S(1)}, u32[]{:S(2)}, u32[]{:S(2)}) collective-permute-start(bf16[128,256]{1,0:T(8,128)(2,1)S(1)} %fusion.7), channel_id=1, source_target_pairs={{0,2},{1,3},{2,4},{3,5},{4,6},{5,7},{6,0},{7,1},{8,10},{9,11},{10,... | collective-permute-start | bytes 196616 | tf_op jit(solution)/shard_map/ppermute | solution.py:44
  32.8 7.8 %collective-permute-start.12 = (bf16[128,256]{1,0:T(8,128)(2,1)S(1)}, bf16[128,256]{1,0:T(8,128)(2,1)S(1)}, u32[]{:S(2)}, u32[]{:S(2)}) collective-permute-start(bf16[128,256]{1,0:T(8,128)(2,1)S(1)} %fusion.7), channel_id=1, source_target_pairs={{0,4},{1,5},{2,6},{3,7},{4,0},{5,1},{6,2},{7,3},{8,12},{9,13},{10,... | collective-permute-start | bytes 196616 | tf_op jit(solution)/shard_map/ppermute | solution.py:44
  35.4 6.0 %collective-permute-start.11 = (bf16[128,256]{1,0:T(8,128)(2,1)S(1)}, bf16[128,256]{1,0:T(8,128)(2,1)S(1)}, u32[]{:S(2)}, u32[]{:S(2)}) collective-permute-start(bf16[128,256]{1,0:T(8,128)(2,1)S(1)} %fusion.7), channel_id=1, source_target_pairs={{0,6},{1,7},{2,0},{3,1},{4,2},{5,3},{6,4},{7,5},{8,14},{9,15},{10,... | collective-permute-start | bytes 196616 | tf_op jit(solution)/shard_map/ppermute | solution.py:44
  36.6 6.1 %collective-permute-start.14 = (bf16[128,256]{1,0:T(8,128)(2,1)S(1)}, bf16[128,256]{1,0:T(8,128)(2,1)S(1)}, u32[]{:S(2)}, u32[]{:S(2)}) collective-permute-start(bf16[128,256]{1,0:T(8,128)(2,1)S(1)} %fusion.7), channel_id=1, source_target_pairs={{0,1},{1,0},{2,3},{3,2},{4,5},{5,4},{6,7},{7,6},{8,9},{9,8},{10,11... | collective-permute-start | bytes 196616 | tf_op jit(solution)/shard_map/ppermute | solution.py:49
  39.3 4.3 %collective-permute-start.17 = (bf16[128,256]{1,0:T(8,128)(2,1)S(1)}, bf16[128,256]{1,0:T(8,128)(2,1)S(1)}, u32[]{:S(2)}, u32[]{:S(2)}) collective-permute-start(bf16[128,256]{1,0:T(8,128)(2,1)S(1)} %collective-permute-done.13), channel_id=1, source_target_pairs={{0,1},{1,0},{2,3},{3,2},{4,5},{5,4},{6,7},{7,6},{8,9},{9,8},{10,11... | collective-permute-start | bytes 196616 | tf_op jit(solution)/shard_map/ppermute | solution.py:49
  40.7 4.3 %collective-permute-start.16 = (bf16[128,256]{1,0:T(8,128)(2,1)S(1)}, bf16[128,256]{1,0:T(8,128)(2,1)S(1)}, u32[]{:S(2)}, u32[]{:S(2)}) collective-permute-start(bf16[128,256]{1,0:T(8,128)(2,1)S(1)} %collective-permute-done.12), channel_id=1, source_target_pairs={{0,1},{1,0},{2,3},{3,2},{4,5},{5,4},{6,7},{7,6},{8,9},{9,8},{10,11... | collective-permute-start | bytes 196616 | tf_op jit(solution)/shard_map/ppermute | solution.py:49
  41.4 4.3 %collective-permute-start.15 = (bf16[128,256]{1,0:T(8,128)(2,1)S(1)}, bf16[128,256]{1,0:T(8,128)(2,1)S(1)}, u32[]{:S(2)}, u32[]{:S(2)}) collective-permute-start(bf16[128,256]{1,0:T(8,128)(2,1)S(1)} %collective-permute-done.11), channel_id=1, source_target_pairs={{0,1},{1,0},{2,3},{3,2},{4,5},{5,4},{6,7},{7,6},{8,9},{9,8},{10,11... | collective-permute-start | bytes 196616 | tf_op jit(solution)/shard_map/ppermute | solution.py:49
  47.6 1.6 %collective-permute-start.18 = (f32[2,128,256]{2,1,0:T(8,128)S(1)}, f32[2,128,256]{2,1,0:T(8,128)S(1)}, u32[]{:S(2)}, u32[]{:S(2)}) collective-permute-start(f32[2,128,256]{2,1,0:T(8,128)S(1)} %dynamic-slice_bitcast_fusion), channel_id=1, source_target_pairs={{0,8},{8,0},{16,24},{24,16},{1,9},{9,1},{17,25},{25,17},{2,10},{10... | collective-permute-start | bytes 786440 | tf_op jit(solution)/shard_map/ppermute | solution.py:76
  49.2 5.6 %collective-permute-start.19 = (f32[128,256]{1,0:T(8,128)S(1)}, f32[128,256]{1,0:T(8,128)S(1)}, u32[]{:S(2)}, u32[]{:S(2)}) collective-permute-start(f32[128,256]{1,0:T(8,128)S(1)} %dynamic-slice_bitcast_fusion.2), channel_id=1, source_target_pairs={{0,16},{8,24},{16,0},{24,8},{1,17},{9,25},{17,1},{25,9},{2,18},{10... | collective-permute-start | bytes 393224 | tf_op jit(solution)/shard_map/ppermute | solution.py:82
  (2 other events, 2.0 us)

commit v5 on v4

--- a/solution.py
+++ b/solution.py
@@ -49,9 +49,7 @@
             full.append(jnp.stack([lax.ppermute(part, axis, perm=perm) for part in outer]))
         else:
             full.append(lax.ppermute(full[0], axis, perm=perm))
-    stacked = jnp.stack(full)
-    order = (lax.iota(jnp.int32, per_tile) - pos) % per_tile
-    return jnp.swapaxes(stacked[order], 0, 1)
+    return jnp.stack(full)
 
 
 def scatter_sum(parts, axis, size):
@@ -65,22 +63,24 @@
 
 
 def scatter_sum_pairs(parts, axis, size):
-    if size % 2:
+    if size % 2 or size == 2:
         return scatter_sum(parts, axis, size)
     me = lax.axis_index(axis)
     low = me % 2
-    by_pair = parts.reshape((size // 2, 2) + parts.shape[1:])
+    pairs = size // 2
+    pair_me = me // 2
+    by_pair = parts.reshape((pairs, 2) + parts.shape[1:])
     mine = lax.dynamic_index_in_dim(by_pair, low, 1, keepdims=False)
     theirs = lax.dynamic_index_in_dim(by_pair, 1 - low, 1, keepdims=False)
-    perm = [(i, i ^ 1) for i in range(size)]
-    half = mine + lax.ppermute(theirs, axis, perm=perm)
-    pair_me = me // 2
-    total = lax.dynamic_index_in_dim(half, pair_me, 0, keepdims=False)
-    for shift in range(1, size // 2):
+    swap = [(i, i ^ 1) for i in range(size)]
+    far = (pair_me + lax.iota(jnp.int32, pairs - 1) + 1) % pairs
+    far_sum = mine[far] + lax.ppermute(theirs[far], axis, perm=swap)
+    near = lax.dynamic_index_in_dim(theirs, pair_me, 0, keepdims=False)
+    total = lax.dynamic_index_in_dim(mine, pair_me, 0, keepdims=False)
+    for shift in range(1, pairs):
         perm = [(i, (i + 2 * shift) % size) for i in range(size)]
-        outgoing = lax.dynamic_index_in_dim(half, (pair_me + shift) % (size // 2), 0, keepdims=False)
-        total = total + lax.ppermute(outgoing, axis, perm=perm)
-    return total
+        total = total + lax.ppermute(far_sum[shift - 1], axis, perm=perm)
+    return total + lax.ppermute(near, axis, perm=swap)
 
 
 def on_device(features, weights, biases, adjacency, tile_row, tile_column, tile_count):
@@ -103,12 +103,11 @@
     placed_lhs = jnp.where(
         slot_mask.reshape(row_tiles, 1, slots * tile_size), lhs[None], jnp.zeros((), lhs.dtype)
     ).reshape(row_tiles * tile_size, slots * tile_size)
-    pick = jnp.broadcast_to(placing[:, None, :, None], (slots, tile_size, row_tiles, 128))
-    row_sums = jnp.dot(
-        lhs, pick.astype(adjacency.dtype).reshape(slots * tile_size, row_tiles * 128),
-        preferred_element_type=jnp.float32,
-    )
-    degree_part = row_sums.reshape(tile_size, row_tiles, 128)[:, :, 0].T.reshape(blk_size, node_dev)
+    ones = jnp.ones((tile_size, 128), adjacency.dtype)
+    slot_sums = jnp.einsum("tij,jk->tik", adjacency, ones, preferred_element_type=jnp.float32)[:, :, 0]
+    degree_part = jnp.sum(
+        jnp.where(placing.T[:, :, None], slot_sums[None], 0.0), axis=1
+    ).reshape(blk_size, node_dev)
     degree = scatter_sum_pairs(degree_part, "blk", blk_size)
     scale = lax.rsqrt(1.0 + degree)[:, None]
     me_grp = lax.axis_index("grp")
@@ -118,9 +117,11 @@
         mixed = jnp.dot(hidden, weights[layer_index], preferred_element_type=jnp.float32)
         scaled = (mixed * scale).astype(jnp.bfloat16)
         if TWO_STAGE_GATHER and per_tile > 1 and grp_size % per_tile == 0:
-            tiles = gather_outer_first(scaled, "grp", grp_size, per_tile, SPLIT)
+            full = gather_outer_first(scaled, "grp", grp_size, per_tile, SPLIT)
             n_tiles = grp_size // per_tile
-            blocks = tiles[(cols_here - me_grp // per_tile) % n_tiles].reshape(slots, tile_size, width)
+            ahead = (cols_here - me_grp // per_tile) % n_tiles
+            from_pos = (lax.iota(jnp.int32, per_tile) - me_grp % per_tile) % per_tile
+            blocks = full[from_pos[None, :], ahead[:, None]].reshape(slots, tile_size, width)
         else:
             received = gather_group(scaled, "grp", grp_size)
             sources = cols_here[:, None] * per_tile + lax.iota(jnp.int32, per_tile)[None, :]

time: 55.7 us -> 55.1 us (0.989)
  local copies, waits for them, and re-layouts: 4.06 us -> 2.8 us
  matrix products: 1.87 us -> 3.02 us
  waiting for transfers between devices: 21.8 us -> 22.4 us
    ppermute x6, waiting for transfers between devices: 2.81 us -> 4.3 us  [gather_outer_first(): outer.append(lax.ppermute(block, axis, perm=perm))]
    ppermute x6, starting transfers between devices: 9.94 us -> 8.61 us  [gather_outer_first(): outer.append(lax.ppermute(block, axis, perm=perm))]
    dot_general x1, matrix products: 0.37 us -> 1.51 us  [on_device(): jnp.einsum('tij,jk->tik', adjacency, ones, preferred_element_type=jnp.flo...]
    gather x4 -> x5, local copies, waits for them, and re-layouts: 2.36 us -> 1.28 us  [the longest x2 1.22 us: on_device(): full[from_pos[None, :], ahead[:, None]].reshape(slots, tile_size, width)]
    ppermute x6 -> x9, starting transfers between devices: 6.72 us -> 7.73 us  [the longest x3 6 us: scatter_sum_pairs(): total = total + lax.ppermute(far_sum[shift - 1], axis, perm=perm)]
    and x2 -> x1, other arithmetic: 0.67 us -> 0.01 us  [on_device(): (rows_here[:, None] == lax.iota(jnp.int32, row_tiles)[None, :]) & live[:,...]
    ppermute x6 -> x9, waiting for transfers between devices: 12.4 us -> 11.9 us  [the longest x3 9.48 us: scatter_sum_pairs(): total = total + lax.ppermute(far_sum[shift - 1], axis, perm=perm)]
  transfers between devices with their start and end apart: 20 -> 23, of which waited for: 15 -> 15; matrix products, arithmetic and copies ran while one was open for 2% -> 3% of each run, Pallas kernels for 0% -> 0%
where the time goes in v5:
time: 55.1 us; the launch traced here: 54.9 us
  starting transfers between devices  24.5 us (44%)
  waiting for transfers between devices  22.4 us (41%)
  matrix products  3.02 us (5%)
  local copies, waits for them, and re-layouts  2.8 us (5%)
  other arithmetic  1.21 us (2%)
  between operations  1.07 us (2%)
    ppermute x3, waiting for transfers between devices, scatter_sum_pairs(): total = total + lax.ppermute(far_sum[shift - 1], axis, perm=perm)  9.48 us
    ppermute x6, starting transfers between devices, gather_outer_first(): outer.append(lax.ppermute(block, axis, perm=perm))  8.61 us
    ppermute x8, starting transfers between devices, gather_outer_first(): lax.ppermute(part, axis, perm=perm)  8.12 us
    ppermute x8, waiting for transfers between devices, gather_outer_first(): lax.ppermute(part, axis, perm=perm)  6.21 us
    ppermute x3, starting transfers between devices, scatter_sum_pairs(): total = total + lax.ppermute(far_sum[shift - 1], axis, perm=perm)  6 us
    ppermute x6, waiting for transfers between devices, gather_outer_first(): outer.append(lax.ppermute(block, axis, perm=perm))  4.3 us
    ppermute x3, waiting for transfers between devices, scatter_sum_pairs(): far_sum = mine[far] + lax.ppermute(theirs[far], axis, perm=swap)  2.37 us
    dot_general x1, matrix products, on_device(): jnp.einsum('tij,jk->tik', adjacency, ones, preferred_element_type=jnp.flo...  1.51 us
  transfers between devices with their start and end apart: 23, of which 15 were waited for; matrix products, arithmetic and copies ran while one was open for 3% of the time, Pallas kernels for 0%

profile of v5, /device:TPU:0, one launch (start us, length us, event | category | flops | bytes accessed | tf_op | source)
XLA Modules:
  0.0 54.9 jit_solution(14798553452243072732)
XLA Ops:
  0.8 1.5 %convolution_bitcast_fusion = f32[6,256,128]{1,2,0:T(8,128)S(1)} fusion(bf16[1,1,6,256,256]{4,3,2,1,0:T(8,128)(2,1)} %param.10), kind=kOutput, calls=%fused_computation.8 | convolution fusion | flops 100663296 | bytes 1572864 | tf_op jit(solution)/shard_map/tij,jk->tik/dot_general | solution.py:107
  3.9 2.8 %collective-permute-start.1 = (f32[128]{0:T(128)S(1)}, f32[128]{0:T(128)S(1)}, u32[]{:S(2)}, u32[]{:S(2)}) collective-permute-start(f32[128]{0:T(128)S(1)} %fusion.49), channel_id=1, source_target_pairs={{0,16},{8,24},{16,0},{24,8},{1,17},{9,25},{17,1},{25,9},{2,18},{10... | collective-permute-start | bytes 1544 | tf_op jit(solution)/shard_map/ppermute | solution.py:82
  6.7 1.4 %collective-permute-done.1 = f32[128]{0:T(128)S(1)} collective-permute-done((f32[128]{0:T(128)S(1)}, f32[128]{0:T(128)S(1)}, u32[]{:S(2)}, u32[]{:S(2)}) %collective-permute-start.1) | collective-permute-done | bytes 544 | tf_op jit(solution)/shard_map/ppermute | solution.py:82
  8.4 4.2 %collective-permute-start.3 = (bf16[128,256]{1,0:T(8,128)(2,1)S(1)}, bf16[128,256]{1,0:T(8,128)(2,1)S(1)}, u32[]{:S(2)}, u32[]{:S(2)}) collective-permute-start(bf16[128,256]{1,0:T(8,128)(2,1)S(1)} %fusion.6), channel_id=1, source_target_pairs={{0,6},{1,7},{2,0},{3,1},{4,2},{5,3},{6,4},{7,5},{8,14},{9,15},{10,... | collective-permute-start | bytes 196616 | tf_op jit(solution)/shard_map/ppermute | solution.py:44
  12.5 1.0 %collective-permute-start.5 = (bf16[128,256]{1,0:T(8,128)(2,1)S(1)}, bf16[128,256]{1,0:T(8,128)(2,1)S(1)}, u32[]{:S(2)}, u32[]{:S(2)}) collective-permute-start(bf16[128,256]{1,0:T(8,128)(2,1)S(1)} %fusion.6), channel_id=1, source_target_pairs={{0,2},{1,3},{2,4},{3,5},{4,6},{5,7},{6,0},{7,1},{8,10},{9,11},{10,... | collective-permute-start | bytes 196616 | tf_op jit(solution)/shard_map/ppermute | solution.py:44
  14.2 0.8 %reshape.308 = bf16[2,128,1536]{2,1,0:T(8,128)(2,1)S(1)} reshape(bf16[256,6,256]{2,1,0:T(8,128)(2,1)S(1)} %copy.12) | data formatting | bytes 1572864 | tf_op jit(solution)/shard_map/jit(_where)/broadcast_in_dim | solution.py:103
  15.1 1.6 %collective-permute-start.6 = (bf16[128,256]{1,0:T(8,128)(2,1)S(1)}, bf16[128,256]{1,0:T(8,128)(2,1)S(1)}, u32[]{:S(2)}, u32[]{:S(2)}) collective-permute-start(bf16[128,256]{1,0:T(8,128)(2,1)S(1)} %fusion.6), channel_id=1, source_target_pairs={{0,1},{1,0},{2,3},{3,2},{4,5},{5,4},{6,7},{7,6},{8,9},{9,8},{10,11... | collective-permute-start | bytes 196616 | tf_op jit(solution)/shard_map/ppermute | solution.py:49
  17.7 1.5 %collective-permute-start.8 = (bf16[128,256]{1,0:T(8,128)(2,1)S(1)}, bf16[128,256]{1,0:T(8,128)(2,1)S(1)}, u32[]{:S(2)}, u32[]{:S(2)}) collective-permute-start(bf16[128,256]{1,0:T(8,128)(2,1)S(1)} %collective-permute-done.4), channel_id=1, source_target_pairs={{0,1},{1,0},{2,3},{3,2},{4,5},{5,4},{6,7},{7,6},{8,9},{9,8},{10,11... | collective-permute-start | bytes 196616 | tf_op jit(solution)/shard_map/ppermute | solution.py:49
  19.2 0.9 %collective-permute-start.9 = (bf16[128,256]{1,0:T(8,128)(2,1)S(1)}, bf16[128,256]{1,0:T(8,128)(2,1)S(1)}, u32[]{:S(2)}, u32[]{:S(2)}) collective-permute-start(bf16[128,256]{1,0:T(8,128)(2,1)S(1)} %collective-permute-done.5), channel_id=1, source_target_pairs={{0,1},{1,0},{2,3},{3,2},{4,5},{5,4},{6,7},{7,6},{8,9},{9,8},{10,11... | collective-permute-start | bytes 196616 | tf_op jit(solution)/shard_map/ppermute | solution.py:49
  20.1 1.2 %collective-permute-done.7 = bf16[128,256]{1,0:T(8,128)(2,1)S(1)} collective-permute-done((bf16[128,256]{1,0:T(8,128)(2,1)S(1)}, bf16[128,256]{1,0:T(8,128)(2,1)S(1)}, u32[]{:S(2)}, u32[]{:S(2)}) %collective-permute-start.7) | collective-permute-done | bytes 65568 | tf_op jit(solution)/shard_map/ppermute | solution.py:49
  21.3 1.0 %collective-permute-done.8 = bf16[128,256]{1,0:T(8,128)(2,1)S(1)} collective-permute-done((bf16[128,256]{1,0:T(8,128)(2,1)S(1)}, bf16[128,256]{1,0:T(8,128)(2,1)S(1)}, u32[]{:S(2)}, u32[]{:S(2)}) %collective-permute-start.8) | collective-permute-done | bytes 65568 | tf_op jit(solution)/shard_map/ppermute | solution.py:49
  22.3 1.2 %collective-permute-done.9 = bf16[128,256]{1,0:T(8,128)(2,1)S(1)} collective-permute-done((bf16[128,256]{1,0:T(8,128)(2,1)S(1)}, bf16[128,256]{1,0:T(8,128)(2,1)S(1)}, u32[]{:S(2)}, u32[]{:S(2)}) %collective-permute-start.9) | collective-permute-done | bytes 65568 | tf_op jit(solution)/shard_map/ppermute | solution.py:49
  25.4 0.8 %collective-permute-done.10 = f32[1,128,256]{2,1,0:T(8,128)S(1)} collective-permute-done((f32[1,128,256]{2,1,0:T(8,128)S(1)}, f32[1,128,256]{2,1,0:T(8,128)S(1)}, u32[]{:S(2)}, u32[]{:S(2)}) %collective-permute-start.10) | collective-permute-done | bytes 131104 | tf_op jit(solution)/shard_map/ppermute | solution.py:77
  26.2 1.6 %collective-permute-start.11 = (f32[128,256]{1,0:T(8,128)S(1)}, f32[128,256]{1,0:T(8,128)S(1)}, u32[]{:S(2)}, u32[]{:S(2)}) collective-permute-start(f32[128,256]{1,0:T(8,128)S(1)} %fusion.20), channel_id=1, source_target_pairs={{0,16},{8,24},{16,0},{24,8},{1,17},{9,25},{17,1},{25,9},{2,18},{10... | collective-permute-start | bytes 393224 | tf_op jit(solution)/shard_map/ppermute | solution.py:82
  27.8 4.0 %collective-permute-done.11 = f32[128,256]{1,0:T(8,128)S(1)} collective-permute-done((f32[128,256]{1,0:T(8,128)S(1)}, f32[128,256]{1,0:T(8,128)S(1)}, u32[]{:S(2)}, u32[]{:S(2)}) %collective-permute-start.11) | collective-permute-done | bytes 131104 | tf_op jit(solution)/shard_map/ppermute | solution.py:82
  32.1 2.6 %collective-permute-start.13 = (bf16[128,256]{1,0:T(8,128)(2,1)S(1)}, bf16[128,256]{1,0:T(8,128)(2,1)S(1)}, u32[]{:S(2)}, u32[]{:S(2)}) collective-permute-start(bf16[128,256]{1,0:T(8,128)(2,1)S(1)} %fusion.7), channel_id=1, source_target_pairs={{0,6},{1,7},{2,0},{3,1},{4,2},{5,3},{6,4},{7,5},{8,14},{9,15},{10,... | collective-permute-start | bytes 196616 | tf_op jit(solution)/shard_map/ppermute | solution.py:44
  34.7 0.8 %collective-permute-start.14 = (bf16[128,256]{1,0:T(8,128)(2,1)S(1)}, bf16[128,256]{1,0:T(8,128)(2,1)S(1)}, u32[]{:S(2)}, u32[]{:S(2)}) collective-permute-start(bf16[128,256]{1,0:T(8,128)(2,1)S(1)} %fusion.7), channel_id=1, source_target_pairs={{0,4},{1,5},{2,6},{3,7},{4,0},{5,1},{6,2},{7,3},{8,12},{9,13},{10,... | collective-permute-start | bytes 196616 | tf_op jit(solution)/shard_map/ppermute | solution.py:44
  35.5 1.0 %collective-permute-start.16 = (bf16[128,256]{1,0:T(8,128)(2,1)S(1)}, bf16[128,256]{1,0:T(8,128)(2,1)S(1)}, u32[]{:S(2)}, u32[]{:S(2)}) collective-permute-start(bf16[128,256]{1,0:T(8,128)(2,1)S(1)} %fusion.7), channel_id=1, source_target_pairs={{0,1},{1,0},{2,3},{3,2},{4,5},{5,4},{6,7},{7,6},{8,9},{9,8},{10,11... | collective-permute-start | bytes 196616 | tf_op jit(solution)/shard_map/ppermute | solution.py:49
  37.7 3.2 %collective-permute-done.14 = bf16[128,256]{1,0:T(8,128)(2,1)S(1)} collective-permute-done((bf16[128,256]{1,0:T(8,128)(2,1)S(1)}, bf16[128,256]{1,0:T(8,128)(2,1)S(1)}, u32[]{:S(2)}, u32[]{:S(2)}) %collective-permute-start.14) | collective-permute-done | bytes 65568 | tf_op jit(solution)/shard_map/ppermute | solution.py:44
  41.6 1.3 %collective-permute-start.19 = (bf16[128,256]{1,0:T(8,128)(2,1)S(1)}, bf16[128,256]{1,0:T(8,128)(2,1)S(1)}, u32[]{:S(2)}, u32[]{:S(2)}) collective-permute-start(bf16[128,256]{1,0:T(8,128)(2,1)S(1)} %collective-permute-done.15), channel_id=1, source_target_pairs={{0,1},{1,0},{2,3},{3,2},{4,5},{5,4},{6,7},{7,6},{8,9},{9,8},{10,11... | collective-permute-start | bytes 196616 | tf_op jit(solution)/shard_map/ppermute | solution.py:49
  43.0 2.2 %collective-permute-done.18 = bf16[128,256]{1,0:T(8,128)(2,1)S(1)} collective-permute-done((bf16[128,256]{1,0:T(8,128)(2,1)S(1)}, bf16[128,256]{1,0:T(8,128)(2,1)S(1)}, u32[]{:S(2)}, u32[]{:S(2)}) %collective-permute-start.18) | collective-permute-done | bytes 65568 | tf_op jit(solution)/shard_map/ppermute | solution.py:49
  47.7 0.8 %collective-permute-done.20 = f32[1,128,256]{2,1,0:T(8,128)S(1)} collective-permute-done((f32[1,128,256]{2,1,0:T(8,128)S(1)}, f32[1,128,256]{2,1,0:T(8,128)S(1)}, u32[]{:S(2)}, u32[]{:S(2)}) %collective-permute-start.20) | collective-permute-done | bytes 131104 | tf_op jit(solution)/shard_map/ppermute | solution.py:77
  48.6 1.6 %collective-permute-start.21 = (f32[128,256]{1,0:T(8,128)S(1)}, f32[128,256]{1,0:T(8,128)S(1)}, u32[]{:S(2)}, u32[]{:S(2)}) collective-permute-start(f32[128,256]{1,0:T(8,128)S(1)} %fusion.13), channel_id=1, source_target_pairs={{0,16},{8,24},{16,0},{24,8},{1,17},{9,25},{17,1},{25,9},{2,18},{10... | collective-permute-start | bytes 393224 | tf_op jit(solution)/shard_map/ppermute | solution.py:82
  50.2 4.0 %collective-permute-done.21 = f32[128,256]{1,0:T(8,128)S(1)} collective-permute-done((f32[128,256]{1,0:T(8,128)S(1)}, f32[128,256]{1,0:T(8,128)S(1)}, u32[]{:S(2)}, u32[]{:S(2)}) %collective-permute-start.21) | collective-permute-done | bytes 131104 | tf_op jit(solution)/shard_map/ppermute | solution.py:82
  (70 shorter events, 10.8 us)
Async XLA Ops:
  0.0 13.7 %copy-start.1 = (bf16[1,1,6,256,256]{4,3,2,1,0:T(8,128)(2,1)S(1)}, bf16[1,1,6,256,256]{4,3,2,1,0:T(8,128)(2,1)}, u32[]{:S(2)}) copy-start(bf16[1,1,6,256,256]{4,3,2,1,0:T(8,128)(2,1)} %param.10) | copy-start | bytes 2359300
  2.5 1.3 %collective-permute-start = (f32[1,128]{1,0:T(1,128)S(1)}, f32[1,128]{1,0:T(1,128)S(1)}, u32[]{:S(2)}, u32[]{:S(2)}) collective-permute-start(f32[1,128]{1,0:T(1,128)S(1)} %get-tuple-element.77), channel_id=1, source_target_pairs={{0,8},{8,0},{16,24},{24,16},{1,9},{9,1},{17,25},{25,17},{2,10},{10... | collective-permute-start | bytes 1544 | tf_op jit(solution)/shard_map/ppermute | solution.py:77
  3.0 3.7 %collective-permute-start.2 = (f32[128]{0:T(128)S(1)}, f32[128]{0:T(128)S(1)}, u32[]{:S(2)}, u32[]{:S(2)}) collective-permute-start(f32[128]{0:T(128)S(1)} %get-tuple-element.78), channel_id=1, source_target_pairs={{0,8},{8,0},{16,24},{24,16},{1,9},{9,1},{17,25},{25,17},{2,10},{10... | collective-permute-start | bytes 1544 | tf_op jit(solution)/shard_map/ppermute | solution.py:83
  3.9 4.3 %collective-permute-start.1 = (f32[128]{0:T(128)S(1)}, f32[128]{0:T(128)S(1)}, u32[]{:S(2)}, u32[]{:S(2)}) collective-permute-start(f32[128]{0:T(128)S(1)} %fusion.49), channel_id=1, source_target_pairs={{0,16},{8,24},{16,0},{24,8},{1,17},{9,25},{17,1},{25,9},{2,18},{10... | collective-permute-start | bytes 1544 | tf_op jit(solution)/shard_map/ppermute | solution.py:82
  8.4 8.2 %collective-permute-start.3 = (bf16[128,256]{1,0:T(8,128)(2,1)S(1)}, bf16[128,256]{1,0:T(8,128)(2,1)S(1)}, u32[]{:S(2)}, u32[]{:S(2)}) collective-permute-start(bf16[128,256]{1,0:T(8,128)(2,1)S(1)} %fusion.6), channel_id=1, source_target_pairs={{0,6},{1,7},{2,0},{3,1},{4,2},{5,3},{6,4},{7,5},{8,14},{9,15},{10,... | collective-permute-start | bytes 196616 | tf_op jit(solution)/shard_map/ppermute | solution.py:44
  12.5 5.2 %collective-permute-start.4 = (bf16[128,256]{1,0:T(8,128)(2,1)S(1)}, bf16[128,256]{1,0:T(8,128)(2,1)S(1)}, u32[]{:S(2)}, u32[]{:S(2)}) collective-permute-start(bf16[128,256]{1,0:T(8,128)(2,1)S(1)} %fusion.6), channel_id=1, source_target_pairs={{0,4},{1,5},{2,6},{3,7},{4,0},{5,1},{6,2},{7,3},{8,12},{9,13},{10,... | collective-permute-start | bytes 196616 | tf_op jit(solution)/shard_map/ppermute | solution.py:44
  12.5 6.7 %collective-permute-start.5 = (bf16[128,256]{1,0:T(8,128)(2,1)S(1)}, bf16[128,256]{1,0:T(8,128)(2,1)S(1)}, u32[]{:S(2)}, u32[]{:S(2)}) collective-permute-start(bf16[128,256]{1,0:T(8,128)(2,1)S(1)} %fusion.6), channel_id=1, source_target_pairs={{0,2},{1,3},{2,4},{3,5},{4,6},{5,7},{6,0},{7,1},{8,10},{9,11},{10,... | collective-permute-start | bytes 196616 | tf_op jit(solution)/shard_map/ppermute | solution.py:44
  15.1 5.1 %collective-permute-start.6 = (bf16[128,256]{1,0:T(8,128)(2,1)S(1)}, bf16[128,256]{1,0:T(8,128)(2,1)S(1)}, u32[]{:S(2)}, u32[]{:S(2)}) collective-permute-start(bf16[128,256]{1,0:T(8,128)(2,1)S(1)} %fusion.6), channel_id=1, source_target_pairs={{0,1},{1,0},{2,3},{3,2},{4,5},{5,4},{6,7},{7,6},{8,9},{9,8},{10,11... | collective-permute-start | bytes 196616 | tf_op jit(solution)/shard_map/ppermute | solution.py:49
  16.6 4.7 %collective-permute-start.7 = (bf16[128,256]{1,0:T(8,128)(2,1)S(1)}, bf16[128,256]{1,0:T(8,128)(2,1)S(1)}, u32[]{:S(2)}, u32[]{:S(2)}) collective-permute-start(bf16[128,256]{1,0:T(8,128)(2,1)S(1)} %collective-permute-done.3), channel_id=1, source_target_pairs={{0,1},{1,0},{2,3},{3,2},{4,5},{5,4},{6,7},{7,6},{8,9},{9,8},{10,11... | collective-permute-start | bytes 196616 | tf_op jit(solution)/shard_map/ppermute | solution.py:49
  17.7 4.6 %collective-permute-start.8 = (bf16[128,256]{1,0:T(8,128)(2,1)S(1)}, bf16[128,256]{1,0:T(8,128)(2,1)S(1)}, u32[]{:S(2)}, u32[]{:S(2)}) collective-permute-start(bf16[128,256]{1,0:T(8,128)(2,1)S(1)} %collective-permute-done.4), channel_id=1, source_target_pairs={{0,1},{1,0},{2,3},{3,2},{4,5},{5,4},{6,7},{7,6},{8,9},{9,8},{10,11... | collective-permute-start | bytes 196616 | tf_op jit(solution)/shard_map/ppermute | solution.py:49
  19.2 4.3 %collective-permute-start.9 = (bf16[128,256]{1,0:T(8,128)(2,1)S(1)}, bf16[128,256]{1,0:T(8,128)(2,1)S(1)}, u32[]{:S(2)}, u32[]{:S(2)}) collective-permute-start(bf16[128,256]{1,0:T(8,128)(2,1)S(1)} %collective-permute-done.5), channel_id=1, source_target_pairs={{0,1},{1,0},{2,3},{3,2},{4,5},{5,4},{6,7},{7,6},{8,9},{9,8},{10,11... | collective-permute-start | bytes 196616 | tf_op jit(solution)/shard_map/ppermute | solution.py:49
  24.8 1.4 %collective-permute-start.10 = (f32[1,128,256]{2,1,0:T(8,128)S(1)}, f32[1,128,256]{2,1,0:T(8,128)S(1)}, u32[]{:S(2)}, u32[]{:S(2)}) collective-permute-start(f32[1,128,256]{2,1,0:T(8,128)S(1)} %get-tuple-element.73), channel_id=1, source_target_pairs={{0,8},{8,0},{16,24},{24,16},{1,9},{9,1},{17,25},{25,17},{2,10},{10... | collective-permute-start | bytes 393224 | tf_op jit(solution)/shard_map/ppermute | solution.py:77
  24.9 3.0 %collective-permute-start.12 = (f32[128,256]{1,0:T(8,128)S(1)}, f32[128,256]{1,0:T(8,128)S(1)}, u32[]{:S(2)}, u32[]{:S(2)}) collective-permute-start(f32[128,256]{1,0:T(8,128)S(1)} %get-tuple-element.74), channel_id=1, source_target_pairs={{0,8},{8,0},{16,24},{24,16},{1,9},{9,1},{17,25},{25,17},{2,10},{10... | collective-permute-start | bytes 393224 | tf_op jit(solution)/shard_map/ppermute | solution.py:83
  26.2 5.6 %collective-permute-start.11 = (f32[128,256]{1,0:T(8,128)S(1)}, f32[128,256]{1,0:T(8,128)S(1)}, u32[]{:S(2)}, u32[]{:S(2)}) collective-permute-start(f32[128,256]{1,0:T(8,128)S(1)} %fusion.20), channel_id=1, source_target_pairs={{0,16},{8,24},{16,0},{24,8},{1,17},{9,25},{17,1},{25,9},{2,18},{10... | collective-permute-start | bytes 393224 | tf_op jit(solution)/shard_map/ppermute | solution.py:82
  32.1 4.9 %collective-permute-start.13 = (bf16[128,256]{1,0:T(8,128)(2,1)S(1)}, bf16[128,256]{1,0:T(8,128)(2,1)S(1)}, u32[]{:S(2)}, u32[]{:S(2)}) collective-permute-start(bf16[128,256]{1,0:T(8,128)(2,1)S(1)} %fusion.7), channel_id=1, source_target_pairs={{0,6},{1,7},{2,0},{3,1},{4,2},{5,3},{6,4},{7,5},{8,14},{9,15},{10,... | collective-permute-start | bytes 196616 | tf_op jit(solution)/shard_map/ppermute | solution.py:44
  34.7 6.2 %collective-permute-start.14 = (bf16[128,256]{1,0:T(8,128)(2,1)S(1)}, bf16[128,256]{1,0:T(8,128)(2,1)S(1)}, u32[]{:S(2)}, u32[]{:S(2)}) collective-permute-start(bf16[128,256]{1,0:T(8,128)(2,1)S(1)} %fusion.7), channel_id=1, source_target_pairs={{0,4},{1,5},{2,6},{3,7},{4,0},{5,1},{6,2},{7,3},{8,12},{9,13},{10,... | collective-permute-start | bytes 196616 | tf_op jit(solution)/shard_map/ppermute | solution.py:44
  35.5 6.1 %collective-permute-start.15 = (bf16[128,256]{1,0:T(8,128)(2,1)S(1)}, bf16[128,256]{1,0:T(8,128)(2,1)S(1)}, u32[]{:S(2)}, u32[]{:S(2)}) collective-permute-start(bf16[128,256]{1,0:T(8,128)(2,1)S(1)} %fusion.7), channel_id=1, source_target_pairs={{0,2},{1,3},{2,4},{3,5},{4,6},{5,7},{6,0},{7,1},{8,10},{9,11},{10,... | collective-permute-start | bytes 196616 | tf_op jit(solution)/shard_map/ppermute | solution.py:44
  35.5 7.4 %collective-permute-start.16 = (bf16[128,256]{1,0:T(8,128)(2,1)S(1)}, bf16[128,256]{1,0:T(8,128)(2,1)S(1)}, u32[]{:S(2)}, u32[]{:S(2)}) collective-permute-start(bf16[128,256]{1,0:T(8,128)(2,1)S(1)} %fusion.7), channel_id=1, source_target_pairs={{0,1},{1,0},{2,3},{3,2},{4,5},{5,4},{6,7},{7,6},{8,9},{9,8},{10,11... | collective-permute-start | bytes 196616 | tf_op jit(solution)/shard_map/ppermute | solution.py:49
  36.9 6.0 %collective-permute-start.17 = (bf16[128,256]{1,0:T(8,128)(2,1)S(1)}, bf16[128,256]{1,0:T(8,128)(2,1)S(1)}, u32[]{:S(2)}, u32[]{:S(2)}) collective-permute-start(bf16[128,256]{1,0:T(8,128)(2,1)S(1)} %collective-permute-done.13), channel_id=1, source_target_pairs={{0,1},{1,0},{2,3},{3,2},{4,5},{5,4},{6,7},{7,6},{8,9},{9,8},{10,11... | collective-permute-start | bytes 196616 | tf_op jit(solution)/shard_map/ppermute | solution.py:49
  40.9 4.3 %collective-permute-start.18 = (bf16[128,256]{1,0:T(8,128)(2,1)S(1)}, bf16[128,256]{1,0:T(8,128)(2,1)S(1)}, u32[]{:S(2)}, u32[]{:S(2)}) collective-permute-start(bf16[128,256]{1,0:T(8,128)(2,1)S(1)} %collective-permute-done.14), channel_id=1, source_target_pairs={{0,1},{1,0},{2,3},{3,2},{4,5},{5,4},{6,7},{7,6},{8,9},{9,8},{10,11... | collective-permute-start | bytes 196616 | tf_op jit(solution)/shard_map/ppermute | solution.py:49
  41.6 4.3 %collective-permute-start.19 = (bf16[128,256]{1,0:T(8,128)(2,1)S(1)}, bf16[128,256]{1,0:T(8,128)(2,1)S(1)}, u32[]{:S(2)}, u32[]{:S(2)}) collective-permute-start(bf16[128,256]{1,0:T(8,128)(2,1)S(1)} %collective-permute-done.15), channel_id=1, source_target_pairs={{0,1},{1,0},{2,3},{3,2},{4,5},{5,4},{6,7},{7,6},{8,9},{9,8},{10,11... | collective-permute-start | bytes 196616 | tf_op jit(solution)/shard_map/ppermute | solution.py:49
  47.2 1.4 %collective-permute-start.20 = (f32[1,128,256]{2,1,0:T(8,128)S(1)}, f32[1,128,256]{2,1,0:T(8,128)S(1)}, u32[]{:S(2)}, u32[]{:S(2)}) collective-permute-start(f32[1,128,256]{2,1,0:T(8,128)S(1)} %get-tuple-element.71), channel_id=1, source_target_pairs={{0,8},{8,0},{16,24},{24,16},{1,9},{9,1},{17,25},{25,17},{2,10},{10... | collective-permute-start | bytes 393224 | tf_op jit(solution)/shard_map/ppermute | solution.py:77
  47.2 2.9 %collective-permute-start.22 = (f32[128,256]{1,0:T(8,128)S(1)}, f32[128,256]{1,0:T(8,128)S(1)}, u32[]{:S(2)}, u32[]{:S(2)}) collective-permute-start(f32[128,256]{1,0:T(8,128)S(1)} %get-tuple-element.72), channel_id=1, source_target_pairs={{0,8},{8,0},{16,24},{24,16},{1,9},{9,1},{17,25},{25,17},{2,10},{10... | collective-permute-start | bytes 393224 | tf_op jit(solution)/shard_map/ppermute | solution.py:83
  48.6 5.6 %collective-permute-start.21 = (f32[128,256]{1,0:T(8,128)S(1)}, f32[128,256]{1,0:T(8,128)S(1)}, u32[]{:S(2)}, u32[]{:S(2)}) collective-permute-start(f32[128,256]{1,0:T(8,128)S(1)} %fusion.13), channel_id=1, source_target_pairs={{0,16},{8,24},{16,0},{24,8},{1,17},{9,25},{17,1},{25,9},{2,18},{10... | collective-permute-start | bytes 393224 | tf_op jit(solution)/shard_map/ppermute | solution.py:82
  (5 other events, 25.5 us)
